TPU v7x, 128 devices: a whole 4x4x4 slice. The times are simulated.
128 devices in a mesh: ctx: 32 (over y, z, core), head: 4 (over x).
Axes of the slice: x: 4, y: 4, z: 4, core: 2. Of those that a mesh axis runs over, the one named last changes fastest.
Arguments:
- mixer_input: bfloat16 [2, 8192, 8192], P(None, 'ctx', 'head'), may hold values from -6 to 6
- gate_input: bfloat16 [2, 8192, 8192], P(None, 'ctx', 'head'), may hold values from -6 to 6
- state_in: bfloat16 [2, 8192, 1024], P(None, 'ctx', 'head'), may hold values from -0.875 to 0.875
- state_out: bfloat16 [2, 8192, 1024], P(None, 'ctx', 'head'), may hold values from -0.875 to 0.875
- step_sizes: float32 [2, 8192, 128], P(None, 'ctx', 'head'), may hold values from 0.5 to 2
- decay_rates: float32 [128], P('head'), may hold values from 3.0517578e-05 to 0.05
- skip_gain: float32 [128], P('head'), may hold values from 0.5 to 2
- norm_gain: float32 [8192], P('head'), may hold values from 0.5 to 1.5
- out_weight: bfloat16 [8192, 4096], P('head', 'ctx'), may hold values from -0.0625 to 0.0625
- queries: bfloat16 [2, 8192, 4096], P(None, 'ctx', 'head'), may hold values from -4.375 to 4.375
- keys: bfloat16 [2, 8192, 1024], P(None, 'ctx', 'head'), may hold values from -4.375 to 4.375
- values: bfloat16 [2, 8192, 1024], P(None, 'ctx', 'head'), may hold values from -6 to 6
- doc_ids: int32 [2, 8192], P(None, 'ctx'), may hold values from 0 to 15, never falling along the last dimension, each value on 1 to 1024 neighbouring positions
Outputs:
- mixer_out: bfloat16 [2, 8192, 4096], P(None, 'ctx', 'head')
- attn_out: bfloat16 [2, 8192, 4096], P(None, 'ctx', 'head')
Inputs may be any that keep to these rules, and one draw needn't show every extreme that they name: `doc_ids`: along each sequence the ids never fall and every id occurs; each document has 1 to 1024 positions, and one document of each sequence has exactly 1024.
All inputs are finite; a program needn't handle non-finite values.
Results may differ from a plain program's by a relative error of at most 0.014.
Values may be sent and summed in bfloat16 or wider, within the bound.
No kernel may reach another device: no remote copies, remote signals or barrier semaphores. Data moves between devices by JAX's collectives and lax.ppermute only.
A program may use at most 256 MiB of HBM per device.

v0:
```python
import jax
import jax.numpy as jnp
from jax import lax
from jax.sharding import PartitionSpec as P

P_SIZE = 64
N = 128
HD = 128
SPAN = 128


epsilon = 1e-05
lowest = -1e30


def shifted(value, axis, by):
    devices = lax.axis_size(axis)
    pairs = [(i, i + by) for i in range(devices) if 0 <= i + by < devices]
    return lax.ppermute(value, axis, pairs)


def link_states(earlier, later):
    decay_one, state_one, first_one, last_one = earlier
    decay_two, state_two, first_two, last_two = later
    passes = ((last_one == first_two) | (last_one < 0.0) | (first_two < 0.0)).astype(jnp.float32)
    through = passes[:, None] * decay_two
    decay = decay_one * through
    state = state_two + through[:, :, None, None] * state_one
    first = jnp.where(first_one < 0.0, first_two, first_one)
    last = jnp.where(last_two < 0.0, last_one, last_two)
    return (decay, state, first, last)


def shards(
    mixer_input,
    gate_input,
    state_in,
    state_out,
    step_sizes,
    decay_rates,
    skip_gain,
    norm_gain,
    out_weight,
    queries,
    keys,
    values,
    doc_ids,
):
    f32 = jnp.float32
    bf16 = jnp.bfloat16
    batches, length, channels = mixer_input.shape
    heads = step_sizes.shape[2]
    groups = state_in.shape[2] // N
    repeat = heads // groups
    count = length // SPAN
    reach = lax.axis_size("ctx") // 8
    position = lax.axis_index("ctx")

    doc_send = doc_ids.astype(bf16)
    arrivals = []
    for offset in range(reach, 0, -1):
        arrivals.append(shifted((keys, values, doc_send), "ctx", offset))

    x = mixer_input.reshape(batches, count, SPAN, heads, P_SIZE)
    dt = step_sizes.reshape(batches, count, SPAN, heads)
    docs = doc_ids.reshape(batches, count, SPAN)
    writers = state_in.reshape(batches, count, SPAN, groups, N)
    readers = state_out.reshape(batches, count, SPAN, groups, N)
    cum = jnp.cumsum(dt * decay_rates, axis=2)
    order = jnp.arange(SPAN, dtype=jnp.int32)
    causal = order[:, None] >= order[None, :]
    allowed = ((docs[:, :, :, None] == docs[:, :, None, :]) & causal)[:, :, None]
    cum_h = jnp.moveaxis(cum, 3, 2)
    spread = cum_h[..., :, None] - cum_h[..., None, :]
    decays = jnp.where(allowed, jnp.exp(-jnp.where(allowed, spread, 0.0)), 0.0)
    intersection = jnp.einsum(
        "bktgn,bksgn->bkgts", readers, writers, preferred_element_type=f32
    )
    intersection = jnp.repeat(intersection, repeat, axis=2)
    dt_h = jnp.moveaxis(dt, 3, 2)
    mixing = (decays * intersection * dt_h[:, :, :, None, :]).astype(bf16)
    within = jnp.einsum(
        "bkhts,bkshp->bkthp", mixing, x, preferred_element_type=f32
    )

    last_doc = docs[:, :, -1]
    ending = cum[:, :, -1:, :] - cum
    tailing = jnp.where((docs == last_doc[:, :, None])[..., None], jnp.exp(-ending), 0.0) * dt
    scaled = (tailing[..., None] * x.astype(f32)).astype(bf16)
    scaled = scaled.reshape(batches, count, SPAN, groups, repeat, P_SIZE)
    written = jnp.einsum(
        "bksgrp,bksgn->bkgrpn", scaled, writers, preferred_element_type=f32
    )
    totals = cum[:, :, -1, :]

    state = written[:, 0]
    block_outs = [within[:, 0]]
    for index in range(1, count):
        living = (docs[:, index] == last_doc[:, index - 1][:, None]).astype(f32)
        carried = jnp.einsum(
            "btgn,bgrpn->btgrp",
            readers[:, index],
            state.astype(bf16),
            preferred_element_type=f32,
        ).reshape(batches, SPAN, heads, P_SIZE)
        carried = carried * (jnp.exp(-cum[:, index]) * living[:, :, None])[..., None]
        block_outs.append(within[:, index] + carried)
        keeping = jnp.exp(-totals[:, index]) * (
            last_doc[:, index] == last_doc[:, index - 1]
        ).astype(f32)[:, None]
        state = state * keeping.reshape(batches, groups, repeat)[..., None, None] + written[:, index]
    local_out = jnp.stack(block_outs, axis=1).reshape(batches, length, heads, P_SIZE)

    cumulative = jnp.cumsum(step_sizes * decay_rates, axis=1)
    first_doc = doc_ids[:, 0]
    end_doc = doc_ids[:, -1]
    passing = jnp.exp(-cumulative[:, -1, :]) * (first_doc == end_doc).astype(f32)[:, None]
    own_state = state.reshape(batches, heads, P_SIZE, N)
    small = jnp.concatenate(
        [passing, first_doc.astype(f32)[:, None], end_doc.astype(f32)[:, None]], axis=1
    )
    received = []
    for offset in range(reach, 0, -1):
        got_small, got_state = shifted((small, own_state.astype(bf16)), "ctx", offset)
        received.append(
            (got_small[:, :heads], got_state.astype(f32), got_small[:, heads], got_small[:, heads + 1])
        )
    before = received[0]
    for item in received[1:]:
        before = link_states(before, item)

    living = (doc_ids.astype(f32) == before[3][:, None]).astype(f32)
    carried = jnp.einsum(
        "btgn,bgrpn->btgrp",
        state_out.reshape(batches, length, groups, N),
        before[1].astype(bf16).reshape(batches, groups, repeat, P_SIZE, N),
        preferred_element_type=f32,
    ).reshape(batches, length, heads, P_SIZE)
    carried = carried * (jnp.exp(-cumulative) * living[:, :, None])[..., None]
    inputs = mixer_input.reshape(batches, length, heads, P_SIZE)
    mixed = local_out + carried + skip_gain[:, None] * inputs.astype(f32)
    gated = mixed.reshape(batches, length, channels) * jax.nn.silu(gate_input.astype(f32))
    shaped = gated.reshape(batches, length, groups, channels // groups)
    factor = lax.rsqrt(jnp.mean(shaped * shaped, axis=-1, keepdims=True) + epsilon)
    normed = ((shaped * factor).reshape(batches, length, channels) * norm_gain).astype(bf16)
    projected = jnp.einsum(
        "btc,cd->btd",
        normed,
        lax.all_gather(out_weight, "ctx", axis=1, tiled=True),
        preferred_element_type=f32,
    )
    mixer_out = lax.psum_scatter(
        projected.astype(bf16), "head", scatter_dimension=2, tiled=True
    )

    kv_heads = keys.shape[2] // HD
    q_repeat = queries.shape[2] // HD // kv_heads
    query_heads = queries.reshape(batches, length, kv_heads, q_repeat, HD)
    window_keys = jnp.concatenate([a[0] for a in arrivals] + [keys], axis=1)
    window_values = jnp.concatenate([a[1] for a in arrivals] + [values], axis=1)
    key_docs = []
    for index, item in enumerate(arrivals):
        offset = reach - index
        key_docs.append(jnp.where(position >= offset, item[2].astype(jnp.int32), -1))
    key_docs = jnp.concatenate(key_docs + [doc_ids], axis=1)
    window = (reach + 1) * length
    query_pos = reach * length + jnp.arange(length, dtype=jnp.int32)
    key_pos = jnp.arange(window, dtype=jnp.int32)
    key_heads = window_keys.reshape(batches, window, kv_heads, HD)
    value_heads = window_values.reshape(batches, window, kv_heads, HD)
    scale = HD ** (-0.5)
    scores = (
        jnp.einsum("bqgrd,bkgd->bgrqk", query_heads, key_heads, preferred_element_type=f32)
        * scale
    )
    allowed = (key_pos[None, :] <= query_pos[:, None])[None] & (
        key_docs[:, None, :] == doc_ids[:, :, None]
    )
    allowed = allowed[:, None, None]
    top = jnp.max(jnp.where(allowed, scores, lowest), axis=-1, keepdims=True)
    probs = jnp.where(allowed, jnp.exp(scores - top), 0.0)
    total = jnp.sum(probs, axis=-1)
    mixed_values = jnp.einsum(
        "bgrqk,bkgd->bgrqd", probs.astype(bf16), value_heads, preferred_element_type=f32
    )
    result = mixed_values / total[..., None]
    attn_out = (
        jnp.transpose(result, (0, 3, 1, 2, 4))
        .reshape(batches, length, kv_heads * q_repeat * HD)
        .astype(bf16)
    )
    return (mixer_out, attn_out)


def solution(mesh):
    in_specs = (
        P(None, "ctx", "head"),
        P(None, "ctx", "head"),
        P(None, "ctx", "head"),
        P(None, "ctx", "head"),
        P(None, "ctx", "head"),
        P("head"),
        P("head"),
        P("head"),
        P("head", "ctx"),
        P(None, "ctx", "head"),
        P(None, "ctx", "head"),
        P(None, "ctx", "head"),
        P(None, "ctx"),
    )
    out_specs = (P(None, "ctx", "head"), P(None, "ctx", "head"))
    return jax.shard_map(shards, mesh=mesh, in_specs=in_specs, out_specs=out_specs, check_vma=False)
```

profile of v0, /device:TPU:9, one launch (start us, length us, event | category | flops | bytes accessed | tf_op | source)
XLA Modules:
  0.0 285.1 jit_solution(17830378582565213450)
XLA Ops:
  12.9 4.1 %collective-permute-start.4 = (f32[2,34]{1,0:T(2,128)}, f32[2,34]{1,0:T(2,128)}, u32[]{:S(2)}, u32[]{:S(2)}) collective-permute-start(f32[2,34]{1,0:T(2,128)} %pad_maximum_fusion.1), channel_id=1, source_target_pairs={{0,4},{4,8},{8,12},{12,16},{16,20},{20,24},{24,28},{28,32},{32,36}... | collective-permute-start | bytes 824 | tf_op jit(solution)/shard_map/ppermute | solution.py:19
  20.5 3.6 %collective-permute-start.3 = (f32[2,34]{1,0:T(2,128)}, f32[2,34]{1,0:T(2,128)}, u32[]{:S(2)}, u32[]{:S(2)}) collective-permute-start(f32[2,34]{1,0:T(2,128)} %pad_maximum_fusion.1), channel_id=1, source_target_pairs={{0,16},{4,20},{8,24},{12,28},{16,32},{20,36},{24,40},{28,44},{32,4... | collective-permute-start | bytes 824 | tf_op jit(solution)/shard_map/ppermute | solution.py:19
  30.0 3.6 %reshape.238 = f32[2,2,128,2,16,64]{2,1,5,4,3,0:T(2,128)} reshape(bf16[2,256,2048]{1,2,0:T(8,128)(2,1)S(1)} %copy.83) | data formatting | bytes 6291456 | tf_op jit(solution)/shard_map/convert_element_type | solution.py:89
  34.5 4.6 %multiply_convert_fusion.2 = bf16[2,2,128,2,16,64]{2,1,5,4,3,0:T(2,128)(2,1)S(1)} fusion(f32[2,2,128,2,16,64]{2,1,5,4,3,0:T(2,128)} %reshape.238, f32[2,2,128,2,16]{2,1,4,3,0:T(2,128)S(1)} %copy.82), kind=kLoop, calls=%fused_computation.32 | loop fusion | flops 2097152 | bytes 6356992 | tf_op jit(solution)/shard_map/convert_element_type | solution.py:89
  43.1 4.3 %collective-permute-start.7 = (bf16[2,32,64,128]{3,2,1,0:T(8,128)(2,1)}, bf16[2,32,64,128]{3,2,1,0:T(8,128)(2,1)}, u32[]{:S(2)}, u32[]{:S(2)}) collective-permute-start(bf16[2,32,64,128]{3,2,1,0:T(8,128)(2,1)} %add_convert_fusion.1), channel_id=1, source_target_pairs={{0,16},{4,20},{8,24},{12,28},{16,32},{20,36},{24,40},{28,44},{32,4... | collective-permute-start | bytes 3145736 | tf_op jit(solution)/shard_map/ppermute | solution.py:19
  47.4 4.4 %collective-permute-start.6 = (bf16[2,32,64,128]{3,2,1,0:T(8,128)(2,1)}, bf16[2,32,64,128]{3,2,1,0:T(8,128)(2,1)}, u32[]{:S(2)}, u32[]{:S(2)}) collective-permute-start(bf16[2,32,64,128]{3,2,1,0:T(8,128)(2,1)} %add_convert_fusion.1), channel_id=1, source_target_pairs={{0,12},{4,16},{8,20},{12,24},{16,28},{20,32},{24,36},{28,40},{32,4... | collective-permute-start | bytes 3145736 | tf_op jit(solution)/shard_map/ppermute | solution.py:19
  51.8 7.1 %reshape.250 = bf16[2,2,128,32,64]{4,3,2,1,0:T(8,128)(2,1)} reshape(bf16[2,256,2048]{2,1,0:T(8,128)(2,1)} %param.13) | data formatting | bytes 4194304 | tf_op jit(solution)/shard_map/reshape | solution.py:64
  64.9 4.6 %fusion.32 = f32[2,2,128,32,64]{2,4,3,1,0:T(8,128)S(1)} fusion(bf16[2,2,128,32,64]{4,3,2,1,0:T(8,128)(2,1)S(1)} %copy-done.3, f32[2,2,32,128,128]{4,3,2,1,0:T(8,128)S(1)} %bitcast.125, f32[2,2,32,128]{3,2,1,0:T(8,128)S(1)} %copy-done.11, f32[2,2,32,128]{3,2,1,0:T(8,128)S(1)} %copy.72, pred[2,2,128,128]{3,2,1,0:T(8,128)(4,1)S(1)} %compare_and_fusion.1), kind=kOutput, calls=%fused_computation.40 | convolution fusion | flops 283115520 | bytes 14876672 | tf_op jit(solution)/shard_map/bkhts,bkshp->bkthp/dot_general | solution.py:82
  77.3 4.0 %copy.93 = bf16[2,256,2048]{1,2,0:T(8,128)(2,1)} copy(bf16[2,256,2048]{2,1,0:T(8,128)(2,1)} %param.14) | data formatting | bytes 4194304 | tf_op args[1]
  81.4 4.4 %collective-permute-start.2 = (f32[2,34]{1,0:T(2,128)}, f32[2,34]{1,0:T(2,128)S(1)}, u32[]{:S(2)}, u32[]{:S(2)}) collective-permute-start(f32[2,34]{1,0:T(2,128)} %pad_maximum_fusion.1), channel_id=1, source_target_pairs={{0,12},{4,16},{8,20},{12,24},{16,28},{20,32},{24,36},{28,40},{32,4... | collective-permute-start | bytes 824 | tf_op jit(solution)/shard_map/ppermute | solution.py:19
  85.9 8.0 %copy.89 = f32[2,2,128,32,64]{2,1,4,3,0:T(2,128)} copy(f32[2,2,128,32,64]{2,4,3,1,0:T(8,128)} %pad_maximum_fusion) | data formatting | bytes 8388608 | tf_op jit(solution)/shard_map/stack | solution.py:112
  93.9 6.4 %reshape.229 = f32[2,256,2048]{1,2,0:T(8,128)} reshape(f32[2,2,128,32,64]{2,1,4,3,0:T(2,128)} %copy.89) | data formatting | bytes 8388608 | tf_op jit(solution)/shard_map/reshape | solution.py:112
  100.3 59.7 %collective-permute-done.2 = f32[2,34]{1,0:T(2,128)S(1)} collective-permute-done((f32[2,34]{1,0:T(2,128)}, f32[2,34]{1,0:T(2,128)S(1)}, u32[]{:S(2)}, u32[]{:S(2)}) %collective-permute-start.2) | collective-permute-done | bytes 304 | tf_op jit(solution)/shard_map/ppermute | solution.py:19
  172.4 13.9 %fusion.12 = bf16[2,256,4096]{2,1,0:T(8,128)(2,1)} fusion(bf16[2,256,2048]{1,2,0:T(8,128)(2,1)S(1)} %fusion.23, bf16[2048,4096]{1,0:T(8,128)(2,1)} %all-gather.2.cloned.1.call-done), kind=kOutput, calls=%fused_computation.15 | convolution fusion | flops 8592031744 | bytes 23068672 | tf_op jit(solution)/shard_map/btc,cd->btd/dot_general | solution.py:146
  189.2 6.4 %collective-permute-start.17 = (bf16[2,256,256]{2,1,0:T(8,128)(2,1)S(1)}, bf16[2,256,256]{2,1,0:T(8,128)(2,1)}, u32[]{:S(2)}, u32[]{:S(2)}) collective-permute-start(bf16[2,256,256]{2,1,0:T(8,128)(2,1)S(1)} %copy-done.9), channel_id=1, source_target_pairs={{0,12},{4,16},{8,20},{12,24},{16,28},{20,32},{24,36},{28,40},{32,4... | collective-permute-start | bytes 786440 | tf_op jit(solution)/shard_map/ppermute | solution.py:19
  195.5 3.7 %collective-permute-start.18 = (bf16[2,256,256]{2,1,0:T(8,128)(2,1)S(1)}, bf16[2,256,256]{2,1,0:T(8,128)(2,1)S(1)}, u32[]{:S(2)}, u32[]{:S(2)}) collective-permute-start(bf16[2,256,256]{2,1,0:T(8,128)(2,1)S(1)} %copy-done.9), channel_id=1, source_target_pairs={{0,8},{4,12},{8,16},{12,20},{16,24},{20,28},{24,32},{28,36},{32,40... | collective-permute-start | bytes 786440 | tf_op jit(solution)/shard_map/ppermute | solution.py:19
  205.9 3.6 %collective-permute-done.8 = bf16[2,256]{1,0:T(2,128)(2,1)S(1)} collective-permute-done((bf16[2,256]{1,0:T(2,128)(2,1)S(1)}, bf16[2,256]{1,0:T(2,128)(2,1)S(1)}, u32[]{:S(2)}, u32[]{:S(2)}) %collective-permute-start.8) | collective-permute-done | bytes 1056 | tf_op jit(solution)/shard_map/ppermute | solution.py:19
  211.8 4.8 %collective-permute-done.9 = bf16[2,256]{1,0:T(2,128)(2,1)S(1)} collective-permute-done((bf16[2,256]{1,0:T(2,128)(2,1)S(1)}, bf16[2,256]{1,0:T(2,128)(2,1)S(1)}, u32[]{:S(2)}, u32[]{:S(2)}) %collective-permute-start.9) | collective-permute-done | bytes 1056 | tf_op jit(solution)/shard_map/ppermute | solution.py:19
  216.6 5.0 %collective-permute-start.10 = (bf16[2,256]{1,0:T(2,128)(2,1)S(1)}, bf16[2,256]{1,0:T(2,128)(2,1)S(1)}, u32[]{:S(2)}, u32[]{:S(2)}) collective-permute-start(bf16[2,256]{1,0:T(2,128)(2,1)S(1)} %convert_element_type.130), channel_id=1, source_target_pairs={{0,8},{4,12},{8,16},{12,20},{16,24},{20,28},{24,32},{28,36},{32,40... | collective-permute-start | bytes 3080 | tf_op jit(solution)/shard_map/ppermute | solution.py:19
  223.0 5.2 %collective-permute-start.11 = (bf16[2,256]{1,0:T(2,128)(2,1)S(1)}, bf16[2,256]{1,0:T(2,128)(2,1)S(1)}, u32[]{:S(2)}, u32[]{:S(2)}) collective-permute-start(bf16[2,256]{1,0:T(2,128)(2,1)S(1)} %convert_element_type.130), channel_id=1, source_target_pairs={{0,4},{4,8},{8,12},{12,16},{16,20},{20,24},{24,28},{28,32},{32,36}... | collective-permute-start | bytes 3080 | tf_op jit(solution)/shard_map/ppermute | solution.py:19
  232.1 8.3 %collective-permute-start.13 = (bf16[2,256,256]{1,2,0:T(8,128)(2,1)S(1)}, bf16[2,256,256]{1,2,0:T(8,128)(2,1)}, u32[]{:S(2)}, u32[]{:S(2)}) collective-permute-start(bf16[2,256,256]{1,2,0:T(8,128)(2,1)S(1)} %copy.95), channel_id=1, source_target_pairs={{0,12},{4,16},{8,20},{12,24},{16,28},{20,32},{24,36},{28,40},{32,4... | collective-permute-start | bytes 786440 | tf_op jit(solution)/shard_map/ppermute | solution.py:19
  249.9 3.9 %collective-permute-done.14 = bf16[2,256,256]{1,2,0:T(8,128)(2,1)} collective-permute-done((bf16[2,256,256]{1,2,0:T(8,128)(2,1)S(1)}, bf16[2,256,256]{1,2,0:T(8,128)(2,1)}, u32[]{:S(2)}, u32[]{:S(2)}) %collective-permute-start.14) | collective-permute-done | bytes 262176 | tf_op jit(solution)/shard_map/ppermute | solution.py:19
  258.0 13.4 %fusion.76 = (f32[2,2,4,256]{3,2,1,0:T(4,128)S(1)}, bf16[2,2,4,256,1280]{3,4,2,1,0:T(8,128)(2,1)}) fusion(pred[2,256,1280]{1,2,0:T(8,128)(4,1)S(1)} %compare_and_fusion, bf16[2,1280,2,128,1]{1,3,4,2,0:T(8,128)(2,1)} %bitcast.137, bf16[2,256,2,4,128]{4,3,2,1,0:T(4,128)(2,1)S(1)} %copy-done.5), kind=kOutput, calls=%fused_computation.133 | convolution fusion | flops 2721056000 | bytes 13516800 | tf_op jit(solution)/shard_map/sub | solution.py:181
  271.4 5.5 %fusion.35 = bf16[2,256,2,4,128]{1,4,3,2,0:T(8,128)(2,1)S(1)} fusion(bf16[2,1280,2,128,1]{1,3,4,2,0:T(8,128)(2,1)S(1)} %bitcast.131, bf16[2,2,4,256,1280]{3,4,2,1,0:T(8,128)(2,1)} %get-tuple-element.23, f32[2,256,2,4]{1,3,2,0:T(4,128)S(1)} %bitcast.143), kind=kOutput, calls=%fused_computation.43 | convolution fusion | flops 1343225856 | bytes 12861440 | tf_op jit(solution)/shard_map/bgrqk,bkgd->bgrqd/dot_general | solution.py:183
  (146 shorter events, 78.0 us)
Async XLA Ops:
  7.2 165.3 %all-gather.2.cloned.1.call-start = ((), (), s32[]{:S(2)}) async-start(), calls=%async_computation.1 | async-start | bytes 17301504 | tf_op jit(solution)/shard_map/all_gather | solution.py:149
  7.9 270.3 %reduce-scatter.2.cloned.1.call-start = ((), (), s32[]{:S(2)}) async-start(), calls=%async_computation.2 | async-start | bytes 5242880 | tf_op jit(solution)/shard_map/reduce_scatter | solution.py:152
  12.9 57.4 %collective-permute-start.4 = (f32[2,34]{1,0:T(2,128)}, f32[2,34]{1,0:T(2,128)}, u32[]{:S(2)}, u32[]{:S(2)}) collective-permute-start(f32[2,34]{1,0:T(2,128)} %pad_maximum_fusion.1), channel_id=1, source_target_pairs={{0,4},{4,8},{8,12},{12,16},{16,20},{20,24},{24,28},{28,32},{32,36}... | collective-permute-start | bytes 824 | tf_op jit(solution)/shard_map/ppermute | solution.py:19
  17.0 55.2 %collective-permute-start.1 = (f32[2,34]{1,0:T(2,128)}, f32[2,34]{1,0:T(2,128)S(1)}, u32[]{:S(2)}, u32[]{:S(2)}) collective-permute-start(f32[2,34]{1,0:T(2,128)} %pad_maximum_fusion.1), channel_id=1, source_target_pairs={{0,8},{4,12},{8,16},{12,20},{16,24},{20,28},{24,32},{28,36},{32,40... | collective-permute-start | bytes 824 | tf_op jit(solution)/shard_map/ppermute | solution.py:19
  20.5 60.8 %collective-permute-start.3 = (f32[2,34]{1,0:T(2,128)}, f32[2,34]{1,0:T(2,128)}, u32[]{:S(2)}, u32[]{:S(2)}) collective-permute-start(f32[2,34]{1,0:T(2,128)} %pad_maximum_fusion.1), channel_id=1, source_target_pairs={{0,16},{4,20},{8,24},{12,28},{16,32},{20,36},{24,40},{28,44},{32,4... | collective-permute-start | bytes 824 | tf_op jit(solution)/shard_map/ppermute | solution.py:19
  43.1 118.9 %collective-permute-start.7 = (bf16[2,32,64,128]{3,2,1,0:T(8,128)(2,1)}, bf16[2,32,64,128]{3,2,1,0:T(8,128)(2,1)}, u32[]{:S(2)}, u32[]{:S(2)}) collective-permute-start(bf16[2,32,64,128]{3,2,1,0:T(8,128)(2,1)} %add_convert_fusion.1), channel_id=1, source_target_pairs={{0,16},{4,20},{8,24},{12,28},{16,32},{20,36},{24,40},{28,44},{32,4... | collective-permute-start | bytes 3145736 | tf_op jit(solution)/shard_map/ppermute | solution.py:19
  47.4 114.6 %collective-permute-start.6 = (bf16[2,32,64,128]{3,2,1,0:T(8,128)(2,1)}, bf16[2,32,64,128]{3,2,1,0:T(8,128)(2,1)}, u32[]{:S(2)}, u32[]{:S(2)}) collective-permute-start(bf16[2,32,64,128]{3,2,1,0:T(8,128)(2,1)} %add_convert_fusion.1), channel_id=1, source_target_pairs={{0,12},{4,16},{8,20},{12,24},{16,28},{20,32},{24,36},{28,40},{32,4... | collective-permute-start | bytes 3145736 | tf_op jit(solution)/shard_map/ppermute | solution.py:19
  70.3 91.7 %collective-permute-start.5 = (bf16[2,32,64,128]{3,2,1,0:T(8,128)(2,1)}, bf16[2,32,64,128]{3,2,1,0:T(8,128)(2,1)}, u32[]{:S(2)}, u32[]{:S(2)}) collective-permute-start(bf16[2,32,64,128]{3,2,1,0:T(8,128)(2,1)} %add_convert_fusion.1), channel_id=1, source_target_pairs={{0,8},{4,12},{8,16},{12,20},{16,24},{20,28},{24,32},{28,36},{32,40... | collective-permute-start | bytes 3145736 | tf_op jit(solution)/shard_map/ppermute | solution.py:19
  72.2 89.8 %collective-permute-start = (bf16[2,32,64,128]{3,2,1,0:T(8,128)(2,1)}, bf16[2,32,64,128]{3,2,1,0:T(8,128)(2,1)}, u32[]{:S(2)}, u32[]{:S(2)}) collective-permute-start(bf16[2,32,64,128]{3,2,1,0:T(8,128)(2,1)} %add_convert_fusion.1), channel_id=1, source_target_pairs={{0,4},{4,8},{8,12},{12,16},{16,20},{20,24},{24,28},{28,32},{32,36}... | collective-permute-start | bytes 3145736 | tf_op jit(solution)/shard_map/ppermute | solution.py:19
  81.4 78.6 %collective-permute-start.2 = (f32[2,34]{1,0:T(2,128)}, f32[2,34]{1,0:T(2,128)S(1)}, u32[]{:S(2)}, u32[]{:S(2)}) collective-permute-start(f32[2,34]{1,0:T(2,128)} %pad_maximum_fusion.1), channel_id=1, source_target_pairs={{0,12},{4,16},{8,20},{12,24},{16,28},{20,32},{24,36},{28,40},{32,4... | collective-permute-start | bytes 824 | tf_op jit(solution)/shard_map/ppermute | solution.py:19
  186.3 17.8 %copy-start.8 = (bf16[2,256,256]{2,1,0:T(8,128)(2,1)S(1)}, bf16[2,256,256]{2,1,0:T(8,128)(2,1)}, u32[]{:S(2)}) copy-start(bf16[2,256,256]{2,1,0:T(8,128)(2,1)} %param.23) | copy-start | bytes 786436
  186.3 18.0 %copy-start.4 = (bf16[2,256,1024]{2,1,0:T(8,128)(2,1)S(1)}, bf16[2,256,1024]{2,1,0:T(8,128)(2,1)}, u32[]{:S(2)}) copy-start(bf16[2,256,1024]{2,1,0:T(8,128)(2,1)} %param.22) | copy-start | bytes 3145732
  187.3 44.8 %collective-permute-start.16 = (bf16[2,256,256]{2,1,0:T(8,128)(2,1)S(1)}, bf16[2,256,256]{2,1,0:T(8,128)(2,1)}, u32[]{:S(2)}, u32[]{:S(2)}) collective-permute-start(bf16[2,256,256]{2,1,0:T(8,128)(2,1)S(1)} %copy-done.9), channel_id=1, source_target_pairs={{0,16},{4,20},{8,24},{12,28},{16,32},{20,36},{24,40},{28,44},{32,4... | collective-permute-start | bytes 786440 | tf_op jit(solution)/shard_map/ppermute | solution.py:19
  189.2 52.1 %collective-permute-start.17 = (bf16[2,256,256]{2,1,0:T(8,128)(2,1)S(1)}, bf16[2,256,256]{2,1,0:T(8,128)(2,1)}, u32[]{:S(2)}, u32[]{:S(2)}) collective-permute-start(bf16[2,256,256]{2,1,0:T(8,128)(2,1)S(1)} %copy-done.9), channel_id=1, source_target_pairs={{0,12},{4,16},{8,20},{12,24},{16,28},{20,32},{24,36},{28,40},{32,4... | collective-permute-start | bytes 786440 | tf_op jit(solution)/shard_map/ppermute | solution.py:19
  195.5 48.7 %collective-permute-start.18 = (bf16[2,256,256]{2,1,0:T(8,128)(2,1)S(1)}, bf16[2,256,256]{2,1,0:T(8,128)(2,1)S(1)}, u32[]{:S(2)}, u32[]{:S(2)}) collective-permute-start(bf16[2,256,256]{2,1,0:T(8,128)(2,1)S(1)} %copy-done.9), channel_id=1, source_target_pairs={{0,8},{4,12},{8,16},{12,20},{16,24},{20,28},{24,32},{28,36},{32,40... | collective-permute-start | bytes 786440 | tf_op jit(solution)/shard_map/ppermute | solution.py:19
  199.3 46.9 %collective-permute-start.19 = (bf16[2,256,256]{2,1,0:T(8,128)(2,1)S(1)}, bf16[2,256,256]{2,1,0:T(8,128)(2,1)S(1)}, u32[]{:S(2)}, u32[]{:S(2)}) collective-permute-start(bf16[2,256,256]{2,1,0:T(8,128)(2,1)S(1)} %copy-done.9), channel_id=1, source_target_pairs={{0,4},{4,8},{8,12},{12,16},{16,20},{20,24},{24,28},{28,32},{32,36}... | collective-permute-start | bytes 786440 | tf_op jit(solution)/shard_map/ppermute | solution.py:19
  201.2 8.2 %collective-permute-start.8 = (bf16[2,256]{1,0:T(2,128)(2,1)S(1)}, bf16[2,256]{1,0:T(2,128)(2,1)S(1)}, u32[]{:S(2)}, u32[]{:S(2)}) collective-permute-start(bf16[2,256]{1,0:T(2,128)(2,1)S(1)} %convert_element_type.130), channel_id=1, source_target_pairs={{0,16},{4,20},{8,24},{12,28},{16,32},{20,36},{24,40},{28,44},{32,4... | collective-permute-start | bytes 3080 | tf_op jit(solution)/shard_map/ppermute | solution.py:19
  209.4 7.1 %collective-permute-start.9 = (bf16[2,256]{1,0:T(2,128)(2,1)S(1)}, bf16[2,256]{1,0:T(2,128)(2,1)S(1)}, u32[]{:S(2)}, u32[]{:S(2)}) collective-permute-start(bf16[2,256]{1,0:T(2,128)(2,1)S(1)} %convert_element_type.130), channel_id=1, source_target_pairs={{0,12},{4,16},{8,20},{12,24},{16,28},{20,32},{24,36},{28,40},{32,4... | collective-permute-start | bytes 3080 | tf_op jit(solution)/shard_map/ppermute | solution.py:19
  216.6 6.4 %collective-permute-start.10 = (bf16[2,256]{1,0:T(2,128)(2,1)S(1)}, bf16[2,256]{1,0:T(2,128)(2,1)S(1)}, u32[]{:S(2)}, u32[]{:S(2)}) collective-permute-start(bf16[2,256]{1,0:T(2,128)(2,1)S(1)} %convert_element_type.130), channel_id=1, source_target_pairs={{0,8},{4,12},{8,16},{12,20},{16,24},{20,28},{24,32},{28,36},{32,40... | collective-permute-start | bytes 3080 | tf_op jit(solution)/shard_map/ppermute | solution.py:19
  223.0 5.9 %collective-permute-start.11 = (bf16[2,256]{1,0:T(2,128)(2,1)S(1)}, bf16[2,256]{1,0:T(2,128)(2,1)S(1)}, u32[]{:S(2)}, u32[]{:S(2)}) collective-permute-start(bf16[2,256]{1,0:T(2,128)(2,1)S(1)} %convert_element_type.130), channel_id=1, source_target_pairs={{0,4},{4,8},{8,12},{12,16},{16,20},{20,24},{24,28},{28,32},{32,36}... | collective-permute-start | bytes 3080 | tf_op jit(solution)/shard_map/ppermute | solution.py:19
  228.9 17.4 %collective-permute-start.12 = (bf16[2,256,256]{1,2,0:T(8,128)(2,1)S(1)}, bf16[2,256,256]{1,2,0:T(8,128)(2,1)S(1)}, u32[]{:S(2)}, u32[]{:S(2)}) collective-permute-start(bf16[2,256,256]{1,2,0:T(8,128)(2,1)S(1)} %copy.95), channel_id=1, source_target_pairs={{0,16},{4,20},{8,24},{12,28},{16,32},{20,36},{24,40},{28,44},{32,4... | collective-permute-start | bytes 786440 | tf_op jit(solution)/shard_map/ppermute | solution.py:19
  232.1 16.1 %collective-permute-start.13 = (bf16[2,256,256]{1,2,0:T(8,128)(2,1)S(1)}, bf16[2,256,256]{1,2,0:T(8,128)(2,1)}, u32[]{:S(2)}, u32[]{:S(2)}) collective-permute-start(bf16[2,256,256]{1,2,0:T(8,128)(2,1)S(1)} %copy.95), channel_id=1, source_target_pairs={{0,12},{4,16},{8,20},{12,24},{16,28},{20,32},{24,36},{28,40},{32,4... | collective-permute-start | bytes 786440 | tf_op jit(solution)/shard_map/ppermute | solution.py:19
  241.3 12.5 %collective-permute-start.14 = (bf16[2,256,256]{1,2,0:T(8,128)(2,1)S(1)}, bf16[2,256,256]{1,2,0:T(8,128)(2,1)}, u32[]{:S(2)}, u32[]{:S(2)}) collective-permute-start(bf16[2,256,256]{1,2,0:T(8,128)(2,1)S(1)} %copy.95), channel_id=1, source_target_pairs={{0,8},{4,12},{8,16},{12,20},{16,24},{20,28},{24,32},{28,36},{32,40... | collective-permute-start | bytes 786440 | tf_op jit(solution)/shard_map/ppermute | solution.py:19
  244.2 11.3 %collective-permute-start.15 = (bf16[2,256,256]{1,2,0:T(8,128)(2,1)S(1)}, bf16[2,256,256]{1,2,0:T(8,128)(2,1)}, u32[]{:S(2)}, u32[]{:S(2)}) collective-permute-start(bf16[2,256,256]{1,2,0:T(8,128)(2,1)S(1)} %copy.95), channel_id=1, source_target_pairs={{0,4},{4,8},{8,12},{12,16},{16,20},{20,24},{24,28},{28,32},{32,36}... | collective-permute-start | bytes 786440 | tf_op jit(solution)/shard_map/ppermute | solution.py:19
  (13 other events, 73.4 us)
Sparse Core Ops, SparseCore 0:
  10.2 162.2 all-gather.1
  186.5 46.7 reduce-scatter.1
where the time goes:
time: 288 us; the launch traced here: 285 us
  waiting for transfers between devices  77.4 us (27%)
  starting transfers between devices  72.7 us (25%)
  local copies, waits for them, and re-layouts  55.3 us (19%)
  matrix products  41.1 us (14%)
  other arithmetic  23.8 us (8%)
  between operations  14.7 us (5%)
    ppermute x20, waiting for transfers between devices, shifted(): return lax.ppermute(value, axis, pairs)  74.6 us
    ppermute x20, starting transfers between devices, shifted(): return lax.ppermute(value, axis, pairs)  72.6 us
    unnamed x43, local copies, waits for them, and re-layouts  21.2 us
    dot_general x1, matrix products, shards(): jnp.einsum('btc,cd->btd', normed, lax.all_gather(out_weight, 'ctx', axis=...  13.9 us
    sub x1, matrix products, shards(): probs = jnp.where(allowed, jnp.exp(scores - top), 0.0)  13.4 us
    another operation x1, local copies, waits for them, and re-layouts, shards(): jnp.stack(block_outs, axis=1).reshape(batches, length, heads, P_SIZE)  8.03 us
    reshape x1, local copies, waits for them, and re-layouts, shards(): x = mixer_input.reshape(batches, count, SPAN, heads, P_SIZE)  7.1 us
    reshape x1, local copies, waits for them, and re-layouts, shards(): jnp.stack(block_outs, axis=1).reshape(batches, length, heads, P_SIZE)  6.42 us
  transfers between devices with their start and end apart: 22, of which 8 were waited for; matrix products, arithmetic and copies ran while one was open for 36% of the time, Pallas kernels for 0%

commit v1 on v0

--- a/solution.py
+++ b/solution.py
@@ -56,10 +56,12 @@
     reach = lax.axis_size("ctx") // 8
     position = lax.axis_index("ctx")
 
-    doc_send = doc_ids.astype(bf16)
+    width = keys.shape[2]
+    doc_row = jnp.pad(doc_ids.astype(bf16), ((0, 0), (0, width)))[:, None, :]
+    payload = jnp.concatenate([jnp.concatenate([keys, values], axis=2), doc_row], axis=1)
     arrivals = []
     for offset in range(reach, 0, -1):
-        arrivals.append(shifted((keys, values, doc_send), "ctx", offset))
+        arrivals.append(shifted(payload, "ctx", offset))
 
     x = mixer_input.reshape(batches, count, SPAN, heads, P_SIZE)
     dt = step_sizes.reshape(batches, count, SPAN, heads)
@@ -82,6 +84,10 @@
     within = jnp.einsum(
         "bkhts,bkshp->bkthp", mixing, x, preferred_element_type=f32
     )
+    arrivals, within = lax.optimization_barrier((arrivals, within))
+    arrivals = [
+        (got[:, :length, :width], got[:, :length, width:], got[:, length, :length]) for got in arrivals
+    ]
 
     last_doc = docs[:, :, -1]
     ending = cum[:, :, -1:, :] - cum

time: 288 us -> 303 us (1.052)
  waiting for transfers between devices: 77.4 us -> 124 us
  starting transfers between devices: 72.7 us -> 38.7 us
  local copies, waits for them, and re-layouts: 55.3 us -> 50.5 us
  matrix products: 41.1 us -> 45.8 us
  other arithmetic: 23.8 us -> 27.5 us
    ppermute x20 -> x12, waiting for transfers between devices: 74.6 us -> 114 us  [shifted(): return lax.ppermute(value, axis, pairs)]
    ppermute x20 -> x12, starting transfers between devices: 72.6 us -> 38.7 us  [shifted(): return lax.ppermute(value, axis, pairs)]
    reduce_scatter x1, waiting for transfers between devices: 0.01 us -> 9.55 us  [shards(): lax.psum_scatter(projected.astype(bf16), 'head', scatter_dimension=2, til...]
    dot_general x1, matrix products: 4.58 us -> 8.38 us  [shards(): jnp.einsum('bkhts,bkshp->bkthp', mixing, x, preferred_element_type=f32)]
    unnamed x43 -> x54, local copies, waits for them, and re-layouts: 21.2 us -> 18.3 us
  transfers between devices with their start and end apart: 22 -> 14, of which waited for: 8 -> 7; matrix products, arithmetic and copies ran while one was open for 36% -> 35% of each run, Pallas kernels for 0% -> 0%
where the time goes in v1:
time: 303 us; the launch traced here: 301 us
  waiting for transfers between devices  124 us (41%)
  local copies, waits for them, and re-layouts  50.5 us (17%)
  matrix products  45.8 us (15%)
  starting transfers between devices  38.7 us (13%)
  other arithmetic  27.5 us (9%)
  between operations  14.7 us (5%)
    ppermute x12, waiting for transfers between devices, shifted(): return lax.ppermute(value, axis, pairs)  114 us
    ppermute x12, starting transfers between devices, shifted(): return lax.ppermute(value, axis, pairs)  38.7 us
    unnamed x54, local copies, waits for them, and re-layouts  18.3 us
    sub x1, matrix products, shards(): probs = jnp.where(allowed, jnp.exp(scores - top), 0.0)  14.3 us
    dot_general x1, matrix products, shards(): jnp.einsum('btc,cd->btd', normed, lax.all_gather(out_weight, 'ctx', axis=...  14 us
    reduce_scatter x1, waiting for transfers between devices, shards(): lax.psum_scatter(projected.astype(bf16), 'head', scatter_dimension=2, til...  9.55 us
    dot_general x1, matrix products, shards(): jnp.einsum('bkhts,bkshp->bkthp', mixing, x, preferred_element_type=f32)  8.38 us
    reshape x1, local copies, waits for them, and re-layouts, shards(): jnp.stack(block_outs, axis=1).reshape(batches, length, heads, P_SIZE)  6.43 us
  transfers between devices with their start and end apart: 14, of which 7 were waited for; matrix products, arithmetic and copies ran while one was open for 35% of the time, Pallas kernels for 0%

profile of v1, /device:TPU:9, one launch (start us, length us, event | category | flops | bytes accessed | tf_op | source)
XLA Modules:
  0.0 301.2 jit_solution(15327045788709965944)
XLA Ops:
  12.9 3.5 %collective-permute-start.5 = (f32[2,34]{1,0:T(2,128)}, f32[2,34]{1,0:T(2,128)S(1)}, u32[]{:S(2)}, u32[]{:S(2)}) collective-permute-start(f32[2,34]{1,0:T(2,128)} %pad_maximum_fusion.2), channel_id=1, source_target_pairs={{0,8},{4,12},{8,16},{12,20},{16,24},{20,28},{24,32},{28,36},{32,40... | collective-permute-start | bytes 824 | tf_op jit(solution)/shard_map/ppermute | solution.py:19
  16.4 6.1 %collective-permute-start.6 = (f32[2,34]{1,0:T(2,128)}, f32[2,34]{1,0:T(2,128)S(1)}, u32[]{:S(2)}, u32[]{:S(2)}) collective-permute-start(f32[2,34]{1,0:T(2,128)} %pad_maximum_fusion.2), channel_id=1, source_target_pairs={{0,12},{4,16},{8,20},{12,24},{16,28},{20,32},{24,36},{28,40},{32,4... | collective-permute-start | bytes 824 | tf_op jit(solution)/shard_map/ppermute | solution.py:19
  31.7 4.9 %collective-permute-start = (bf16[2,257,512]{2,0,1:T(2,128)(2,1)}, bf16[2,257,512]{2,0,1:T(2,128)(2,1)}, u32[]{:S(2)}, u32[]{:S(2)}) collective-permute-start(bf16[2,257,512]{2,0,1:T(2,128)(2,1)} %pad_maximum_fusion.1), channel_id=1, source_target_pairs={{0,16},{4,20},{8,24},{12,28},{16,32},{20,36},{24,40},{28,44},{32,4... | collective-permute-start | bytes 1579016 | tf_op jit(solution)/shard_map/ppermute | solution.py:19
  36.7 5.3 %reshape.266 = bf16[2,2,128,32,64]{4,3,2,1,0:T(8,128)(2,1)} reshape(bf16[2,256,2048]{2,1,0:T(8,128)(2,1)S(1)} %copy-done.1) | data formatting | bytes 4194304 | tf_op jit(solution)/shard_map/reshape | solution.py:66
  48.5 3.6 %reshape.254 = f32[2,2,128,2,16,64]{2,1,5,4,3,0:T(2,128)} reshape(bf16[2,256,2048]{1,2,0:T(8,128)(2,1)S(1)} %copy.95) | data formatting | bytes 6291456 | tf_op jit(solution)/shard_map/convert_element_type | solution.py:95
  53.2 4.5 %multiply_convert_fusion.2 = bf16[2,2,128,2,16,64]{2,1,5,4,3,0:T(2,128)(2,1)S(1)} fusion(f32[2,2,128,2,16,64]{2,1,5,4,3,0:T(2,128)} %reshape.254, f32[2,2,128,2,16]{2,1,4,3,0:T(2,128)S(1)} %copy.94), kind=kLoop, calls=%fused_computation.32 | loop fusion | flops 2097152 | bytes 6356992 | tf_op jit(solution)/shard_map/convert_element_type | solution.py:95
  64.7 8.4 %fusion.32 = f32[2,2,128,32,64]{2,4,3,1,0:T(8,128)} fusion(bf16[2,2,128,32,64]{4,3,2,1,0:T(8,128)(2,1)S(1)} %copy-done.3, f32[2,2,32,128,128]{4,3,2,1,0:T(8,128)S(1)} %bitcast.135, f32[2,2,32,128]{3,2,1,0:T(8,128)S(1)} %copy-done.17, f32[2,2,32,128]{3,2,1,0:T(8,128)S(1)} %copy.84, pred[2,2,128,128]{3,2,1,0:T(8,128)(4,1)S(1)} %compare_and_fusion.1), kind=kOutput, calls=%fused_computation.40 | convolution fusion | flops 283115520 | bytes 14876672 | tf_op jit(solution)/shard_map/bkhts,bkshp->bkthp/dot_general | solution.py:84
  73.1 4.0 %copy.105 = bf16[2,256,2048]{1,2,0:T(8,128)(2,1)} copy(bf16[2,256,2048]{2,1,0:T(8,128)(2,1)} %param.14) | data formatting | bytes 4194304 | tf_op args[1]
  80.4 3.7 %collective-permute-start.2 = (bf16[2,257,512]{2,0,1:T(2,128)(2,1)}, bf16[2,257,512]{2,0,1:T(2,128)(2,1)S(1)}, u32[]{:S(2)}, u32[]{:S(2)}) collective-permute-start(bf16[2,257,512]{2,0,1:T(2,128)(2,1)} %pad_maximum_fusion.1), channel_id=1, source_target_pairs={{0,8},{4,12},{8,16},{12,20},{16,24},{20,28},{24,32},{28,36},{32,40... | collective-permute-start | bytes 1579016 | tf_op jit(solution)/shard_map/ppermute | solution.py:19
  86.1 4.0 %collective-permute-start.10 = (bf16[2,32,64,128]{3,2,1,0:T(8,128)(2,1)}, bf16[2,32,64,128]{3,2,1,0:T(8,128)(2,1)}, u32[]{:S(2)}, u32[]{:S(2)}) collective-permute-start(bf16[2,32,64,128]{3,2,1,0:T(8,128)(2,1)} %add_convert_fusion.1), channel_id=1, source_target_pairs={{0,12},{4,16},{8,20},{12,24},{16,28},{20,32},{24,36},{28,40},{32,4... | collective-permute-start | bytes 3145736 | tf_op jit(solution)/shard_map/ppermute | solution.py:19
  93.6 12.9 %collective-permute-done.1 = bf16[2,257,512]{2,0,1:T(2,128)(2,1)S(1)} collective-permute-done((bf16[2,257,512]{2,0,1:T(2,128)(2,1)}, bf16[2,257,512]{2,0,1:T(2,128)(2,1)S(1)}, u32[]{:S(2)}, u32[]{:S(2)}) %collective-permute-start.1) | collective-permute-done | bytes 526368 | tf_op jit(solution)/shard_map/ppermute | solution.py:19
  108.4 21.9 %collective-permute-done.2 = bf16[2,257,512]{2,0,1:T(2,128)(2,1)S(1)} collective-permute-done((bf16[2,257,512]{2,0,1:T(2,128)(2,1)}, bf16[2,257,512]{2,0,1:T(2,128)(2,1)S(1)}, u32[]{:S(2)}, u32[]{:S(2)}) %collective-permute-start.2) | collective-permute-done | bytes 526368 | tf_op jit(solution)/shard_map/ppermute | solution.py:19
  133.4 3.6 %fusion.74 = (f32[2,1,128,32,64]{2,4,3,1,0:T(8,128)S(1)}, f32[2,1,128,32,64]{2,4,3,1,0:T(8,128)S(1)}) fusion(f32[2,2,128,32,64]{2,4,3,1,0:T(8,128)} %fusion.32, f32[2,1,128,32,64]{2,4,3,1,0:T(8,128)} %bitcast.134, f32[2,128,32]{1,2,0:T(8,128)S(1)} %copy.100), kind=kLoop, calls=%fused_computation.133 | loop fusion | flops 1048576 | bytes 10518528 | tf_op jit(solution)/shard_map/slice | solution.py:103
  137.4 5.8 %copy.101 = f32[2,2,128,32,64]{2,1,4,3,0:T(2,128)} copy(f32[2,2,128,32,64]{2,4,3,1,0:T(8,128)S(1)} %pad_maximum_fusion) | data formatting | bytes 8388608 | tf_op jit(solution)/shard_map/stack | solution.py:118
  143.2 6.4 %reshape.245 = f32[2,256,2048]{1,2,0:T(8,128)} reshape(f32[2,2,128,32,64]{2,1,4,3,0:T(2,128)} %copy.101) | data formatting | bytes 8388608 | tf_op jit(solution)/shard_map/reshape | solution.py:118
  149.6 17.3 %collective-permute-done.10 = bf16[2,32,64,128]{3,2,1,0:T(8,128)(2,1)} collective-permute-done((bf16[2,32,64,128]{3,2,1,0:T(8,128)(2,1)}, bf16[2,32,64,128]{3,2,1,0:T(8,128)(2,1)}, u32[]{:S(2)}, u32[]{:S(2)}) %collective-permute-start.10) | collective-permute-done | bytes 1048608 | tf_op jit(solution)/shard_map/ppermute | solution.py:19
  167.0 8.8 %collective-permute-done.11 = bf16[2,32,64,128]{3,2,1,0:T(8,128)(2,1)} collective-permute-done((bf16[2,32,64,128]{3,2,1,0:T(8,128)(2,1)}, bf16[2,32,64,128]{3,2,1,0:T(8,128)(2,1)}, u32[]{:S(2)}, u32[]{:S(2)}) %collective-permute-start.11) | collective-permute-done | bytes 1048608 | tf_op jit(solution)/shard_map/ppermute | solution.py:19
  175.8 16.8 %collective-permute-done.4 = bf16[2,32,64,128]{3,2,1,0:T(8,128)(2,1)} collective-permute-done((bf16[2,32,64,128]{3,2,1,0:T(8,128)(2,1)}, bf16[2,32,64,128]{3,2,1,0:T(8,128)(2,1)}, u32[]{:S(2)}, u32[]{:S(2)}) %collective-permute-start.4) | collective-permute-done | bytes 1048608 | tf_op jit(solution)/shard_map/ppermute | solution.py:19
  192.6 36.0 %collective-permute-done.9 = bf16[2,32,64,128]{3,2,1,0:T(8,128)(2,1)} collective-permute-done((bf16[2,32,64,128]{3,2,1,0:T(8,128)(2,1)}, bf16[2,32,64,128]{3,2,1,0:T(8,128)(2,1)}, u32[]{:S(2)}, u32[]{:S(2)}) %collective-permute-start.9) | collective-permute-done | bytes 1048608 | tf_op jit(solution)/shard_map/ppermute | solution.py:19
  228.6 3.3 %add_convert_fusion = bf16[2,32,64,128]{3,2,1,0:T(8,128)(2,1)S(1)} fusion(bf16[2,32,64,128]{3,2,1,0:T(8,128)(2,1)} %collective-permute-done.11, bf16[2,32,64,128]{3,2,1,0:T(8,128)(2,1)} %collective-permute-done.10, bf16[2,32,64,128]{3,2,1,0:T(8,128)(2,1)} %collective-permute-done.9, bf16[2,32,64,128]{3,2,1,0:T(8,128)(2,1)} %collective-permute-done.4, ...), kind=kLoop, calls=%fused_computation.45 | loop fusion | flops 5767168 | bytes 5243648 | tf_op jit(solution)/shard_map/convert_element_type | solution.py:142
  236.9 14.0 %fusion.12 = bf16[2,256,4096]{2,1,0:T(8,128)(2,1)} fusion(bf16[2,256,2048]{1,2,0:T(8,128)(2,1)S(1)} %fusion.23, bf16[2048,4096]{1,0:T(8,128)(2,1)} %all-gather.2.cloned.1.call-done), kind=kOutput, calls=%fused_computation.15 | convolution fusion | flops 8592031744 | bytes 23068672 | tf_op jit(solution)/shard_map/btc,cd->btd/dot_general | solution.py:152
  263.6 14.3 %fusion.76 = (f32[2,2,4,256]{3,2,1,0:T(4,128)S(1)}, bf16[2,2,4,256,1280]{3,4,2,1,0:T(8,128)(2,1)}) fusion(pred[2,256,1280]{1,2,0:T(8,128)(4,1)S(1)} %compare_and_fusion, bf16[2,1280,2,128,1]{1,3,4,2,0:T(8,128)(2,1)} %bitcast.142, bf16[2,256,2,4,128]{4,3,2,1,0:T(4,128)(2,1)} %reshape.252), kind=kOutput, calls=%fused_computation.135 | convolution fusion | flops 2721056000 | bytes 13516800 | tf_op jit(solution)/shard_map/sub | solution.py:187
  277.9 5.6 %fusion.35 = bf16[2,256,2,4,128]{1,4,3,2,0:T(8,128)(2,1)S(1)} fusion(bf16[2,1280,2,128,1]{1,3,4,2,0:T(8,128)(2,1)S(1)} %bitcast.141, bf16[2,2,4,256,1280]{3,4,2,1,0:T(8,128)(2,1)} %get-tuple-element.41, f32[2,256,2,4]{1,3,2,0:T(4,128)S(1)} %bitcast.153), kind=kOutput, calls=%fused_computation.42 | convolution fusion | flops 1343225856 | bytes 12861440 | tf_op jit(solution)/shard_map/bgrqk,bkgd->bgrqd/dot_general | solution.py:189
  284.8 9.6 %reduce-scatter.2.cloned.1.call-done = bf16[2,256,1024]{2,1,0:T(8,128)(2,1)} async-done(((bf16[2,256,4096]{2,1,0:T(8,128)(2,1)}), bf16[2,256,1024]{2,1,0:T(8,128)(2,1)}) %reduce-scatter.2.cloned.1.call-update) | async-done | bytes 1048592 | tf_op jit(solution)/shard_map/reduce_scatter | solution.py:158
  (144 shorter events, 62.2 us)
Async XLA Ops:
  7.2 29.5 %copy-start.9 = (f32[2,256,32]{1,2,0:T(8,128)S(1)}, f32[2,256,32]{1,2,0:T(8,128)}, u32[]{:S(2)}) copy-start(f32[2,256,32]{1,2,0:T(8,128)} %param.17) | copy-start | bytes 196612
  7.2 29.5 %copy-start.16 = (s32[2,256]{1,0:T(2,128)S(1)}, s32[2,256]{1,0:T(2,128)}, u32[]{:S(2)}) copy-start(s32[2,256]{1,0:T(2,128)} %param.25) | copy-start | bytes 6148
  7.2 29.6 %copy-start.1 = (bf16[2,256,2048]{2,1,0:T(8,128)(2,1)S(1)}, bf16[2,256,2048]{2,1,0:T(8,128)(2,1)}, u32[]{:S(2)}) copy-start(bf16[2,256,2048]{2,1,0:T(8,128)(2,1)} %param.13) | copy-start | bytes 6291460
  7.2 229.7 %all-gather.2.cloned.1.call-start = ((), (), s32[]{:S(2)}) async-start(), calls=%async_computation.1 | async-start | bytes 17301504 | tf_op jit(solution)/shard_map/all_gather | solution.py:155
  7.9 286.5 %reduce-scatter.2.cloned.1.call-start = ((), (), s32[]{:S(2)}) async-start(), calls=%async_computation.2 | async-start | bytes 5242880 | tf_op jit(solution)/shard_map/reduce_scatter | solution.py:158
  12.9 64.3 %collective-permute-start.5 = (f32[2,34]{1,0:T(2,128)}, f32[2,34]{1,0:T(2,128)S(1)}, u32[]{:S(2)}, u32[]{:S(2)}) collective-permute-start(f32[2,34]{1,0:T(2,128)} %pad_maximum_fusion.2), channel_id=1, source_target_pairs={{0,8},{4,12},{8,16},{12,20},{16,24},{20,28},{24,32},{28,36},{32,40... | collective-permute-start | bytes 824 | tf_op jit(solution)/shard_map/ppermute | solution.py:19
  16.4 64.0 %collective-permute-start.6 = (f32[2,34]{1,0:T(2,128)}, f32[2,34]{1,0:T(2,128)S(1)}, u32[]{:S(2)}, u32[]{:S(2)}) collective-permute-start(f32[2,34]{1,0:T(2,128)} %pad_maximum_fusion.2), channel_id=1, source_target_pairs={{0,12},{4,16},{8,20},{12,24},{16,28},{20,32},{24,36},{28,40},{32,4... | collective-permute-start | bytes 824 | tf_op jit(solution)/shard_map/ppermute | solution.py:19
  22.5 61.7 %collective-permute-start.8 = (f32[2,34]{1,0:T(2,128)}, f32[2,34]{1,0:T(2,128)S(1)}, u32[]{:S(2)}, u32[]{:S(2)}) collective-permute-start(f32[2,34]{1,0:T(2,128)} %pad_maximum_fusion.2), channel_id=1, source_target_pairs={{0,4},{4,8},{8,12},{12,16},{16,20},{20,24},{24,28},{28,32},{32,36}... | collective-permute-start | bytes 824 | tf_op jit(solution)/shard_map/ppermute | solution.py:19
  24.4 61.7 %collective-permute-start.7 = (f32[2,34]{1,0:T(2,128)}, f32[2,34]{1,0:T(2,128)}, u32[]{:S(2)}, u32[]{:S(2)}) collective-permute-start(f32[2,34]{1,0:T(2,128)} %pad_maximum_fusion.2), channel_id=1, source_target_pairs={{0,16},{4,20},{8,24},{12,28},{16,32},{20,36},{24,40},{28,44},{32,4... | collective-permute-start | bytes 824 | tf_op jit(solution)/shard_map/ppermute | solution.py:19
  31.7 59.4 %collective-permute-start = (bf16[2,257,512]{2,0,1:T(2,128)(2,1)}, bf16[2,257,512]{2,0,1:T(2,128)(2,1)}, u32[]{:S(2)}, u32[]{:S(2)}) collective-permute-start(bf16[2,257,512]{2,0,1:T(2,128)(2,1)} %pad_maximum_fusion.1), channel_id=1, source_target_pairs={{0,16},{4,20},{8,24},{12,28},{16,32},{20,36},{24,40},{28,44},{32,4... | collective-permute-start | bytes 1579016 | tf_op jit(solution)/shard_map/ppermute | solution.py:19
  42.1 3.2 %copy-start.20 = (f32[32]{0:T(128)S(1)}, f32[32]{0:T(128)}, u32[]{:S(2)}) copy-start(f32[32]{0:T(128)} %param.18) | copy-start | bytes 388
  45.1 7.9 %copy-start.4 = (bf16[2,2,128,2,128]{4,3,2,1,0:T(2,128)(2,1)}, bf16[2,2,128,2,128]{4,3,2,1,0:T(2,128)(2,1)S(1)}, u32[]{:S(2)}) copy-start(bf16[2,2,128,2,128]{4,3,2,1,0:T(2,128)(2,1)S(1)} %reshape.239) | copy-start | bytes 786436
  48.5 4.1 %copy-start.19 = (f32[2,2,1,32]{3,2,1,0:T(1,128)S(1)}, f32[2,2,1,32]{3,2,1,0:T(1,128)}, u32[]{:S(2)}) copy-start(f32[2,2,1,32]{3,2,1,0:T(1,128)} %get-tuple-element.36) | copy-start | bytes 1540
  73.1 4.0 %copy-start.21 = (f32[32]{0:T(128)S(1)}, f32[32]{0:T(128)}, u32[]{:S(2)}) copy-start(f32[32]{0:T(128)} %param.19) | copy-start | bytes 388
  77.2 29.3 %collective-permute-start.1 = (bf16[2,257,512]{2,0,1:T(2,128)(2,1)}, bf16[2,257,512]{2,0,1:T(2,128)(2,1)S(1)}, u32[]{:S(2)}, u32[]{:S(2)}) collective-permute-start(bf16[2,257,512]{2,0,1:T(2,128)(2,1)} %pad_maximum_fusion.1), channel_id=1, source_target_pairs={{0,12},{4,16},{8,20},{12,24},{16,28},{20,32},{24,36},{28,40},{32,4... | collective-permute-start | bytes 1579016 | tf_op jit(solution)/shard_map/ppermute | solution.py:19
  80.4 49.9 %collective-permute-start.2 = (bf16[2,257,512]{2,0,1:T(2,128)(2,1)}, bf16[2,257,512]{2,0,1:T(2,128)(2,1)S(1)}, u32[]{:S(2)}, u32[]{:S(2)}) collective-permute-start(bf16[2,257,512]{2,0,1:T(2,128)(2,1)} %pad_maximum_fusion.1), channel_id=1, source_target_pairs={{0,8},{4,12},{8,16},{12,20},{16,24},{20,28},{24,32},{28,36},{32,40... | collective-permute-start | bytes 1579016 | tf_op jit(solution)/shard_map/ppermute | solution.py:19
  84.2 48.5 %collective-permute-start.3 = (bf16[2,257,512]{2,0,1:T(2,128)(2,1)}, bf16[2,257,512]{2,0,1:T(2,128)(2,1)S(1)}, u32[]{:S(2)}, u32[]{:S(2)}) collective-permute-start(bf16[2,257,512]{2,0,1:T(2,128)(2,1)} %pad_maximum_fusion.1), channel_id=1, source_target_pairs={{0,4},{4,8},{8,12},{12,16},{16,20},{20,24},{24,28},{28,32},{32,36}... | collective-permute-start | bytes 1579016 | tf_op jit(solution)/shard_map/ppermute | solution.py:19
  86.1 80.9 %collective-permute-start.10 = (bf16[2,32,64,128]{3,2,1,0:T(8,128)(2,1)}, bf16[2,32,64,128]{3,2,1,0:T(8,128)(2,1)}, u32[]{:S(2)}, u32[]{:S(2)}) collective-permute-start(bf16[2,32,64,128]{3,2,1,0:T(8,128)(2,1)} %add_convert_fusion.1), channel_id=1, source_target_pairs={{0,12},{4,16},{8,20},{12,24},{16,28},{20,32},{24,36},{28,40},{32,4... | collective-permute-start | bytes 3145736 | tf_op jit(solution)/shard_map/ppermute | solution.py:19
  91.1 84.7 %collective-permute-start.11 = (bf16[2,32,64,128]{3,2,1,0:T(8,128)(2,1)}, bf16[2,32,64,128]{3,2,1,0:T(8,128)(2,1)}, u32[]{:S(2)}, u32[]{:S(2)}) collective-permute-start(bf16[2,32,64,128]{3,2,1,0:T(8,128)(2,1)} %add_convert_fusion.1), channel_id=1, source_target_pairs={{0,16},{4,20},{8,24},{12,28},{16,32},{20,36},{24,40},{28,44},{32,4... | collective-permute-start | bytes 3145736 | tf_op jit(solution)/shard_map/ppermute | solution.py:19
  106.5 30.6 %copy-start.10 = (bf16[2,257,512]{2,0,1:T(2,128)(2,1)}, bf16[2,257,512]{2,0,1:T(2,128)(2,1)S(1)}, u32[]{:S(2)}) copy-start(bf16[2,257,512]{2,0,1:T(2,128)(2,1)S(1)} %collective-permute-done.1) | copy-start | bytes 1579012
  106.5 86.1 %collective-permute-start.4 = (bf16[2,32,64,128]{3,2,1,0:T(8,128)(2,1)}, bf16[2,32,64,128]{3,2,1,0:T(8,128)(2,1)}, u32[]{:S(2)}, u32[]{:S(2)}) collective-permute-start(bf16[2,32,64,128]{3,2,1,0:T(8,128)(2,1)} %add_convert_fusion.1), channel_id=1, source_target_pairs={{0,4},{4,8},{8,12},{12,16},{16,20},{20,24},{24,28},{28,32},{32,36}... | collective-permute-start | bytes 3145736 | tf_op jit(solution)/shard_map/ppermute | solution.py:19
  130.3 98.2 %collective-permute-start.9 = (bf16[2,32,64,128]{3,2,1,0:T(8,128)(2,1)}, bf16[2,32,64,128]{3,2,1,0:T(8,128)(2,1)}, u32[]{:S(2)}, u32[]{:S(2)}) collective-permute-start(bf16[2,32,64,128]{3,2,1,0:T(8,128)(2,1)} %add_convert_fusion.1), channel_id=1, source_target_pairs={{0,8},{4,12},{8,16},{12,20},{16,24},{20,28},{24,32},{28,36},{32,40... | collective-permute-start | bytes 3145736 | tf_op jit(solution)/shard_map/ppermute | solution.py:19
  228.6 4.0 %copy-start.2 = (bf16[2,256,2048]{1,2,0:T(8,128)(2,1)S(1)}, bf16[2,256,2048]{1,2,0:T(8,128)(2,1)}, u32[]{:S(2)}) copy-start(bf16[2,256,2048]{1,2,0:T(8,128)(2,1)} %copy.105) | copy-start | bytes 6291460
  250.9 4.5 %copy-start.11 = (bf16[2,257,512]{2,0,1:T(2,128)(2,1)S(1)}, bf16[2,257,512]{2,0,1:T(2,128)(2,1)}, u32[]{:S(2)}) copy-start(bf16[2,257,512]{2,0,1:T(2,128)(2,1)} %copy-done.10) | copy-start | bytes 1579012
  (13 other events, 27.7 us)
Sparse Core Ops, SparseCore 0:
  10.2 165.6 all-gather.1
  251.0 43.3 reduce-scatter.1

commit v2 on v1

--- a/solution.py
+++ b/solution.py
@@ -155,9 +155,10 @@
         lax.all_gather(out_weight, "ctx", axis=1, tiled=True),
         preferred_element_type=f32,
     )
-    mixer_out = lax.psum_scatter(
-        projected.astype(bf16), "head", scatter_dimension=2, tiled=True
-    )
+    parts = lax.axis_size("head")
+    pieces = projected.astype(bf16).reshape(batches, length, parts, -1)
+    pieces = lax.all_to_all(pieces, "head", 2, 2, tiled=True)
+    mixer_out = jnp.sum(pieces.astype(f32), axis=2).astype(bf16)
 
     kv_heads = keys.shape[2] // HD
     q_repeat = queries.shape[2] // HD // kv_heads

time: 303 us -> 330 us (1.089)
  waiting for transfers between devices: 124 us -> 108 us
  local copies, waits for them, and re-layouts: 50.5 us -> 64.7 us
  other arithmetic: 27.5 us -> 40.8 us
  matrix products: 45.8 us -> 53 us
  starting transfers between devices: 38.7 us -> 44.1 us
    ppermute x12, waiting for transfers between devices: 114 us -> 89.8 us  [shifted(): return lax.ppermute(value, axis, pairs)]
    all_to_all x0 -> x1, waiting for transfers between devices: none -> 17.2 us  [shards(): pieces = lax.all_to_all(pieces, 'head', 2, 2, tiled=True)]
    reduce_scatter x1 -> x0, waiting for transfers between devices: 9.55 us -> none  [shards(): lax.psum_scatter(projected.astype(bf16), 'head', scatter_dimension=2, til...]
    dot_general x1, matrix products: 14 us -> 22 us  [shards(): jnp.einsum('btc,cd->btd', normed, lax.all_gather(out_weight, 'ctx', axis=...]
    all_to_all x0 -> x1, starting transfers between devices: none -> 4.99 us  [shards(): pieces = lax.all_to_all(pieces, 'head', 2, 2, tiled=True)]
    reduce_sum x0 -> x1, other arithmetic: none -> 4.39 us  [shards(): mixer_out = jnp.sum(pieces.astype(f32), axis=2).astype(bf16)]
    unnamed x54 -> x74, local copies, waits for them, and re-layouts: 18.3 us -> 18.8 us
  transfers between devices with their start and end apart: 14 -> 14, of which waited for: 7 -> 7; matrix products, arithmetic and copies ran while one was open for 35% -> 38% of each run, Pallas kernels for 0% -> 0%
where the time goes in v2:
time: 330 us; the launch traced here: 325 us
  waiting for transfers between devices  108 us (33%)
  local copies, waits for them, and re-layouts  64.7 us (20%)
  matrix products  53 us (16%)
  starting transfers between devices  44.1 us (13%)
  other arithmetic  40.8 us (12%)
  between operations  14.8 us (4%)
    ppermute x12, waiting for transfers between devices, shifted(): return lax.ppermute(value, axis, pairs)  89.8 us
    ppermute x12, starting transfers between devices, shifted(): return lax.ppermute(value, axis, pairs)  39.1 us
    dot_general x1, matrix products, shards(): jnp.einsum('btc,cd->btd', normed, lax.all_gather(out_weight, 'ctx', axis=...  22 us
    unnamed x74, local copies, waits for them, and re-layouts  18.8 us
    all_to_all x1, waiting for transfers between devices, shards(): pieces = lax.all_to_all(pieces, 'head', 2, 2, tiled=True)  17.2 us
    sub x1, matrix products, shards(): probs = jnp.where(allowed, jnp.exp(scores - top), 0.0)  13.6 us
    dot_general x1, matrix products, shards(): jnp.einsum('bkhts,bkshp->bkthp', mixing, x, preferred_element_type=f32)  8.38 us
    another operation x1, local copies, waits for them, and re-layouts, shards(): jnp.stack(block_outs, axis=1).reshape(batches, length, heads, P_SIZE)  8.03 us
  transfers between devices with their start and end apart: 14, of which 7 were waited for; matrix products, arithmetic and copies ran while one was open for 38% of the time, Pallas kernels for 0%

profile of v2, /device:TPU:9, one launch (start us, length us, event | category | flops | bytes accessed | tf_op | source)
XLA Modules:
  0.0 325.0 jit_solution(17962374838078539993)
XLA Ops:
  12.9 3.5 %collective-permute-start.5 = (f32[2,34]{1,0:T(2,128)}, f32[2,34]{1,0:T(2,128)}, u32[]{:S(2)}, u32[]{:S(2)}) collective-permute-start(f32[2,34]{1,0:T(2,128)} %pad_maximum_fusion.2), channel_id=1, source_target_pairs={{0,8},{4,12},{8,16},{12,20},{16,24},{20,28},{24,32},{28,36},{32,40... | collective-permute-start | bytes 824 | tf_op jit(solution)/shard_map/ppermute | solution.py:19
  16.4 6.1 %collective-permute-start.6 = (f32[2,34]{1,0:T(2,128)}, f32[2,34]{1,0:T(2,128)}, u32[]{:S(2)}, u32[]{:S(2)}) collective-permute-start(f32[2,34]{1,0:T(2,128)} %pad_maximum_fusion.2), channel_id=1, source_target_pairs={{0,12},{4,16},{8,20},{12,24},{16,28},{20,32},{24,36},{28,40},{32,4... | collective-permute-start | bytes 824 | tf_op jit(solution)/shard_map/ppermute | solution.py:19
  31.0 4.9 %collective-permute-start = (bf16[2,257,512]{2,0,1:T(2,128)(2,1)S(1)}, bf16[2,257,512]{2,0,1:T(2,128)(2,1)}, u32[]{:S(2)}, u32[]{:S(2)}) collective-permute-start(bf16[2,257,512]{2,0,1:T(2,128)(2,1)S(1)} %pad_maximum_fusion.1), channel_id=1, source_target_pairs={{0,16},{4,20},{8,24},{12,28},{16,32},{20,36},{24,40},{28,44},{32,4... | collective-permute-start | bytes 1579016 | tf_op jit(solution)/shard_map/ppermute | solution.py:19
  36.6 5.3 %reshape.270 = bf16[2,2,128,32,64]{4,3,2,1,0:T(8,128)(2,1)} reshape(bf16[2,256,2048]{2,1,0:T(8,128)(2,1)S(1)} %copy-done.1) | data formatting | bytes 4194304 | tf_op jit(solution)/shard_map/reshape | solution.py:66
  56.2 3.6 %reshape.258 = f32[2,2,128,2,16,64]{2,1,5,4,3,0:T(2,128)} reshape(bf16[2,256,2048]{1,2,0:T(8,128)(2,1)S(1)} %copy.129) | data formatting | bytes 6291456 | tf_op jit(solution)/shard_map/convert_element_type | solution.py:95
  63.7 4.6 %multiply_convert_fusion.2 = bf16[2,2,128,2,16,64]{2,1,5,4,3,0:T(2,128)(2,1)S(1)} fusion(f32[2,2,128,2,16,64]{2,1,5,4,3,0:T(2,128)} %reshape.258, f32[2,2,128,2,16]{2,1,4,3,0:T(2,128)S(1)} %copy.128), kind=kLoop, calls=%fused_computation.33 | loop fusion | flops 2097152 | bytes 6356992 | tf_op jit(solution)/shard_map/convert_element_type | solution.py:95
  76.9 8.4 %fusion.32 = f32[2,2,128,32,64]{2,4,3,1,0:T(8,128)} fusion(bf16[2,2,128,32,64]{4,3,2,1,0:T(8,128)(2,1)S(1)} %copy-done.4, f32[2,2,32,128,128]{4,3,2,1,0:T(8,128)S(1)} %bitcast.140, f32[2,2,32,128]{3,2,1,0:T(8,128)S(1)} %copy-done.22, f32[2,2,32,128]{3,2,1,0:T(8,128)S(1)} %copy-done.21, pred[2,2,128,128]{3,2,1,0:T(8,128)(4,1)S(1)} %compare_and_fusion.1), kind=kOutput, calls=%fused_computation.41 | convolution fusion | flops 283115520 | bytes 14876672 | tf_op jit(solution)/shard_map/bkhts,bkshp->bkthp/dot_general | solution.py:84
  85.3 4.0 %copy.139 = bf16[2,256,2048]{1,2,0:T(8,128)(2,1)} copy(bf16[2,256,2048]{2,1,0:T(8,128)(2,1)} %param.14) | data formatting | bytes 4194304 | tf_op args[1]
  89.4 3.2 collective-permute-start.1
  97.6 4.9 %collective-permute-start.10 = (bf16[2,32,64,128]{3,2,1,0:T(8,128)(2,1)}, bf16[2,32,64,128]{3,2,1,0:T(8,128)(2,1)}, u32[]{:S(2)}, u32[]{:S(2)}) collective-permute-start(bf16[2,32,64,128]{3,2,1,0:T(8,128)(2,1)} %add_convert_fusion.1), channel_id=1, source_target_pairs={{0,12},{4,16},{8,20},{12,24},{16,28},{20,32},{24,36},{28,40},{32,4... | collective-permute-start | bytes 3145736 | tf_op jit(solution)/shard_map/ppermute | solution.py:19
  109.6 4.8 %collective-permute-done.1 = bf16[2,257,512]{2,0,1:T(2,128)(2,1)S(1)} collective-permute-done((bf16[2,257,512]{2,0,1:T(2,128)(2,1)S(1)}, bf16[2,257,512]{2,0,1:T(2,128)(2,1)S(1)}, u32[]{:S(2)}, u32[]{:S(2)}) %collective-permute-start.1) | collective-permute-done | bytes 526368 | tf_op jit(solution)/shard_map/ppermute | solution.py:19
  116.5 21.9 %collective-permute-done.2 = bf16[2,257,512]{2,0,1:T(2,128)(2,1)S(1)} collective-permute-done((bf16[2,257,512]{2,0,1:T(2,128)(2,1)S(1)}, bf16[2,257,512]{2,0,1:T(2,128)(2,1)S(1)}, u32[]{:S(2)}, u32[]{:S(2)}) %collective-permute-start.2) | collective-permute-done | bytes 526368 | tf_op jit(solution)/shard_map/ppermute | solution.py:19
  153.2 3.3 %copy.147 = bf16[2,1280,256]{1,2,0:T(8,128)(2,1)S(1)} copy(bf16[2,1280,256]{2,0,1:T(2,128)(2,1)} %copy-done.5) | data formatting | bytes 2621440 | tf_op jit(solution)/shard_map/concatenate | solution.py:167
  156.6 8.0 %copy.135 = f32[2,2,128,32,64]{2,1,4,3,0:T(2,128)} copy(f32[2,2,128,32,64]{2,4,3,1,0:T(8,128)} %pad_maximum_fusion) | data formatting | bytes 8388608 | tf_op jit(solution)/shard_map/stack | solution.py:118
  164.6 6.4 %reshape.248 = f32[2,256,2048]{1,2,0:T(8,128)} reshape(f32[2,2,128,32,64]{2,1,4,3,0:T(2,128)} %copy.135) | data formatting | bytes 8388608 | tf_op jit(solution)/shard_map/reshape | solution.py:118
  176.8 16.8 %collective-permute-done.4 = bf16[2,32,64,128]{3,2,1,0:T(8,128)(2,1)} collective-permute-done((bf16[2,32,64,128]{3,2,1,0:T(8,128)(2,1)}, bf16[2,32,64,128]{3,2,1,0:T(8,128)(2,1)}, u32[]{:S(2)}, u32[]{:S(2)}) %collective-permute-start.4) | collective-permute-done | bytes 1048608 | tf_op jit(solution)/shard_map/ppermute | solution.py:19
  193.6 43.0 %collective-permute-done.9 = bf16[2,32,64,128]{3,2,1,0:T(8,128)(2,1)} collective-permute-done((bf16[2,32,64,128]{3,2,1,0:T(8,128)(2,1)}, bf16[2,32,64,128]{3,2,1,0:T(8,128)(2,1)}, u32[]{:S(2)}, u32[]{:S(2)}) %collective-permute-start.9) | collective-permute-done | bytes 1048608 | tf_op jit(solution)/shard_map/ppermute | solution.py:19
  236.7 3.3 %add_convert_fusion = bf16[2,32,64,128]{3,2,1,0:T(8,128)(2,1)S(1)} fusion(bf16[2,32,64,128]{3,2,1,0:T(8,128)(2,1)} %collective-permute-done.11, bf16[2,32,64,128]{3,2,1,0:T(8,128)(2,1)} %collective-permute-done.10, bf16[2,32,64,128]{3,2,1,0:T(8,128)(2,1)} %collective-permute-done.9, bf16[2,32,64,128]{3,2,1,0:T(8,128)(2,1)} %collective-permute-done.4, ...), kind=kLoop, calls=%fused_computation.46 | loop fusion | flops 5767168 | bytes 5243648 | tf_op jit(solution)/shard_map/convert_element_type | solution.py:142
  245.0 22.0 %fusion.12 = bf16[2,256,4096]{2,1,0:T(8,128)(2,1)S(1)} fusion(bf16[2,256,2048]{1,2,0:T(8,128)(2,1)S(1)} %fusion.23, bf16[2048,4096]{1,0:T(8,128)(2,1)} %all-gather.2.cloned.1.call-done), kind=kOutput, calls=%fused_computation.15 | convolution fusion | flops 8592031744 | bytes 23068672 | tf_op jit(solution)/shard_map/btc,cd->btd/dot_general | solution.py:152
  269.5 5.0 %all-to-all-start = ((bf16[2,256,4,1024]{3,1,0,2:T(8,128)(2,1)}), bf16[2,256,4,1024]{3,1,0,2:T(8,128)(2,1)}, u32[]{:S(2)}, u32[]{:S(2)}) async-start(bf16[2,256,4,1024]{3,1,0,2:T(8,128)(2,1)} %bitcast.138), calls=%async_computation | async-start | bytes 8388608 | tf_op jit(solution)/shard_map/all_to_all | solution.py:160
  275.9 13.6 %fusion.76 = (f32[2,2,4,256]{3,2,1,0:T(4,128)S(1)}, bf16[2,2,4,256,1280]{3,4,2,1,0:T(8,128)(2,1)}) fusion(pred[2,256,1280]{1,2,0:T(8,128)(4,1)} %compare_and_fusion, bf16[2,1280,2,128,1]{1,3,4,2,0:T(8,128)(2,1)S(1)} %bitcast.148, bf16[2,256,2,4,128]{4,3,2,1,0:T(4,128)(2,1)} %reshape.256), kind=kOutput, calls=%fused_computation.136 | convolution fusion | flops 2721056000 | bytes 13516800 | tf_op jit(solution)/shard_map/sub | solution.py:188
  289.5 5.5 %fusion.35 = bf16[2,256,2,4,128]{1,4,3,2,0:T(8,128)(2,1)S(1)} fusion(bf16[2,1280,2,128,1]{1,3,4,2,0:T(8,128)(2,1)S(1)} %bitcast.147, bf16[2,2,4,256,1280]{3,4,2,1,0:T(8,128)(2,1)} %get-tuple-element.43, f32[2,256,2,4]{1,3,2,0:T(4,128)S(1)} %bitcast.159), kind=kOutput, calls=%fused_computation.43 | convolution fusion | flops 1343225856 | bytes 12861440 | tf_op jit(solution)/shard_map/bgrqk,bkgd->bgrqd/dot_general | solution.py:190
  296.4 17.2 %all-to-all-done = bf16[2,256,4,1024]{3,1,0,2:T(8,128)(2,1)} async-done(((bf16[2,256,4,1024]{3,1,0,2:T(8,128)(2,1)}), bf16[2,256,4,1024]{3,1,0,2:T(8,128)(2,1)}, u32[]{:S(2)}, u32[]{:S(2)}) %all-to-all-start) | async-done | bytes 4194336 | tf_op jit(solution)/shard_map/all_to_all | solution.py:160
  313.6 4.4 %reduce_sum.31 = bf16[2,256,1024]{2,1,0:T(8,128)(2,1)} reduce(bf16[2,256,4,1024]{3,1,0,2:T(8,128)(2,1)} %all-to-all-done, bf16[]{:T(256)} %constant.16.clone.1), dimensions={2}, to_apply=%region_4.5 | reduce | flops 1572864 | bytes 5242882 | tf_op jit(solution)/shard_map/reduce_sum | solution.py:161
  (165 shorter events, 86.3 us)
Async XLA Ops:
  7.2 28.7 %copy-start.13 = (f32[2,256,32]{1,2,0:T(8,128)S(1)}, f32[2,256,32]{1,2,0:T(8,128)}, u32[]{:S(2)}) copy-start(f32[2,256,32]{1,2,0:T(8,128)} %param.17) | copy-start | bytes 196612
  7.2 28.8 %copy-start.20 = (s32[2,256]{1,0:T(2,128)S(1)}, s32[2,256]{1,0:T(2,128)}, u32[]{:S(2)}) copy-start(s32[2,256]{1,0:T(2,128)} %param.25) | copy-start | bytes 6148
  7.2 29.4 %copy-start.1 = (bf16[2,256,2048]{2,1,0:T(8,128)(2,1)S(1)}, bf16[2,256,2048]{2,1,0:T(8,128)(2,1)}, u32[]{:S(2)}) copy-start(bf16[2,256,2048]{2,1,0:T(8,128)(2,1)} %param.13) | copy-start | bytes 6291460
  7.2 237.8 %all-gather.2.cloned.1.call-start = ((), (), s32[]{:S(2)}) async-start(), calls=%async_computation.1 | async-start | bytes 17301504 | tf_op jit(solution)/shard_map/all_gather | solution.py:155
  12.9 76.6 %collective-permute-start.5 = (f32[2,34]{1,0:T(2,128)}, f32[2,34]{1,0:T(2,128)}, u32[]{:S(2)}, u32[]{:S(2)}) collective-permute-start(f32[2,34]{1,0:T(2,128)} %pad_maximum_fusion.2), channel_id=1, source_target_pairs={{0,8},{4,12},{8,16},{12,20},{16,24},{20,28},{24,32},{28,36},{32,40... | collective-permute-start | bytes 824 | tf_op jit(solution)/shard_map/ppermute | solution.py:19
  16.4 76.3 %collective-permute-start.6 = (f32[2,34]{1,0:T(2,128)}, f32[2,34]{1,0:T(2,128)}, u32[]{:S(2)}, u32[]{:S(2)}) collective-permute-start(f32[2,34]{1,0:T(2,128)} %pad_maximum_fusion.2), channel_id=1, source_target_pairs={{0,12},{4,16},{8,20},{12,24},{16,28},{20,32},{24,36},{28,40},{32,4... | collective-permute-start | bytes 824 | tf_op jit(solution)/shard_map/ppermute | solution.py:19
  22.5 73.1 %collective-permute-start.8 = (f32[2,34]{1,0:T(2,128)}, f32[2,34]{1,0:T(2,128)}, u32[]{:S(2)}, u32[]{:S(2)}) collective-permute-start(f32[2,34]{1,0:T(2,128)} %pad_maximum_fusion.2), channel_id=1, source_target_pairs={{0,4},{4,8},{8,12},{12,16},{16,20},{20,24},{24,28},{28,32},{32,36}... | collective-permute-start | bytes 824 | tf_op jit(solution)/shard_map/ppermute | solution.py:19
  24.4 73.2 %collective-permute-start.7 = (f32[2,34]{1,0:T(2,128)}, f32[2,34]{1,0:T(2,128)}, u32[]{:S(2)}, u32[]{:S(2)}) collective-permute-start(f32[2,34]{1,0:T(2,128)} %pad_maximum_fusion.2), channel_id=1, source_target_pairs={{0,16},{4,20},{8,24},{12,28},{16,32},{20,36},{24,40},{28,44},{32,4... | collective-permute-start | bytes 824 | tf_op jit(solution)/shard_map/ppermute | solution.py:19
  31.0 75.9 %collective-permute-start = (bf16[2,257,512]{2,0,1:T(2,128)(2,1)S(1)}, bf16[2,257,512]{2,0,1:T(2,128)(2,1)}, u32[]{:S(2)}, u32[]{:S(2)}) collective-permute-start(bf16[2,257,512]{2,0,1:T(2,128)(2,1)S(1)} %pad_maximum_fusion.1), channel_id=1, source_target_pairs={{0,16},{4,20},{8,24},{12,28},{16,32},{20,36},{24,40},{28,44},{32,4... | collective-permute-start | bytes 1579016 | tf_op jit(solution)/shard_map/ppermute | solution.py:19
  85.3 20.9 %copy-start.24 = (f32[2,32,2]{1,2,0:T(2,128)S(1)}, f32[2,32,2]{1,2,0:T(2,128)}, u32[]{:S(2)}) copy-start(f32[2,32,2]{1,2,0:T(2,128)} %copy-done.23) | copy-start | bytes 1540
  89.4 24.9 %collective-permute-start.1 = (bf16[2,257,512]{2,0,1:T(2,128)(2,1)S(1)}, bf16[2,257,512]{2,0,1:T(2,128)(2,1)S(1)}, u32[]{:S(2)}, u32[]{:S(2)}) collective-permute-start(bf16[2,257,512]{2,0,1:T(2,128)(2,1)S(1)} %pad_maximum_fusion.1), channel_id=1, source_target_pairs={{0,12},{4,16},{8,20},{12,24},{16,28},{20,32},{24,36},{28,40},{32,4... | collective-permute-start | bytes 1579016 | tf_op jit(solution)/shard_map/ppermute | solution.py:19
  92.7 45.8 %collective-permute-start.2 = (bf16[2,257,512]{2,0,1:T(2,128)(2,1)S(1)}, bf16[2,257,512]{2,0,1:T(2,128)(2,1)S(1)}, u32[]{:S(2)}, u32[]{:S(2)}) collective-permute-start(bf16[2,257,512]{2,0,1:T(2,128)(2,1)S(1)} %pad_maximum_fusion.1), channel_id=1, source_target_pairs={{0,8},{4,12},{8,16},{12,20},{16,24},{20,28},{24,32},{28,36},{32,40... | collective-permute-start | bytes 1579016 | tf_op jit(solution)/shard_map/ppermute | solution.py:19
  95.6 44.8 %collective-permute-start.3 = (bf16[2,257,512]{2,0,1:T(2,128)(2,1)S(1)}, bf16[2,257,512]{2,0,1:T(2,128)(2,1)S(1)}, u32[]{:S(2)}, u32[]{:S(2)}) collective-permute-start(bf16[2,257,512]{2,0,1:T(2,128)(2,1)S(1)} %pad_maximum_fusion.1), channel_id=1, source_target_pairs={{0,4},{4,8},{8,12},{12,16},{16,20},{20,24},{24,28},{28,32},{32,36}... | collective-permute-start | bytes 1579016 | tf_op jit(solution)/shard_map/ppermute | solution.py:19
  97.6 77.5 %collective-permute-start.10 = (bf16[2,32,64,128]{3,2,1,0:T(8,128)(2,1)}, bf16[2,32,64,128]{3,2,1,0:T(8,128)(2,1)}, u32[]{:S(2)}, u32[]{:S(2)}) collective-permute-start(bf16[2,32,64,128]{3,2,1,0:T(8,128)(2,1)} %add_convert_fusion.1), channel_id=1, source_target_pairs={{0,12},{4,16},{8,20},{12,24},{16,28},{20,32},{24,36},{28,40},{32,4... | collective-permute-start | bytes 3145736 | tf_op jit(solution)/shard_map/ppermute | solution.py:19
  106.9 36.4 %copy-start.10 = (bf16[2,256,256]{2,1,0:T(8,128)(2,1)S(1)}, bf16[2,256,256]{2,1,0:T(8,128)(2,1)}, u32[]{:S(2)}) copy-start(bf16[2,256,256]{2,1,0:T(8,128)(2,1)} %param.24) | copy-start | bytes 786436
  106.9 36.4 %copy-start.11 = (bf16[2,256,256]{2,1,0:T(8,128)(2,1)S(1)}, bf16[2,256,256]{2,1,0:T(8,128)(2,1)}, u32[]{:S(2)}) copy-start(bf16[2,256,256]{2,1,0:T(8,128)(2,1)} %param.23) | copy-start | bytes 786436
  106.9 69.9 %collective-permute-start.11 = (bf16[2,32,64,128]{3,2,1,0:T(8,128)(2,1)}, bf16[2,32,64,128]{3,2,1,0:T(8,128)(2,1)}, u32[]{:S(2)}, u32[]{:S(2)}) collective-permute-start(bf16[2,32,64,128]{3,2,1,0:T(8,128)(2,1)} %add_convert_fusion.1), channel_id=1, source_target_pairs={{0,16},{4,20},{8,24},{12,28},{16,32},{20,36},{24,40},{28,44},{32,4... | collective-permute-start | bytes 3145736 | tf_op jit(solution)/shard_map/ppermute | solution.py:19
  114.3 28.9 %copy-start.14 = (bf16[2,257,512]{2,0,1:T(2,128)(2,1)}, bf16[2,257,512]{2,0,1:T(2,128)(2,1)S(1)}, u32[]{:S(2)}) copy-start(bf16[2,257,512]{2,0,1:T(2,128)(2,1)S(1)} %collective-permute-done.1) | copy-start | bytes 1579012
  114.4 79.3 %collective-permute-start.4 = (bf16[2,32,64,128]{3,2,1,0:T(8,128)(2,1)}, bf16[2,32,64,128]{3,2,1,0:T(8,128)(2,1)}, u32[]{:S(2)}, u32[]{:S(2)}) collective-permute-start(bf16[2,32,64,128]{3,2,1,0:T(8,128)(2,1)} %add_convert_fusion.1), channel_id=1, source_target_pairs={{0,4},{4,8},{8,12},{12,16},{16,20},{20,24},{24,28},{28,32},{32,36}... | collective-permute-start | bytes 3145736 | tf_op jit(solution)/shard_map/ppermute | solution.py:19
  138.5 98.2 %collective-permute-start.9 = (bf16[2,32,64,128]{3,2,1,0:T(8,128)(2,1)}, bf16[2,32,64,128]{3,2,1,0:T(8,128)(2,1)}, u32[]{:S(2)}, u32[]{:S(2)}) collective-permute-start(bf16[2,32,64,128]{3,2,1,0:T(8,128)(2,1)} %add_convert_fusion.1), channel_id=1, source_target_pairs={{0,8},{4,12},{8,16},{12,20},{16,24},{20,28},{24,32},{28,36},{32,40... | collective-permute-start | bytes 3145736 | tf_op jit(solution)/shard_map/ppermute | solution.py:19
  164.6 72.1 %copy-start.27 = (f32[2,32]{1,0:T(2,128)S(1)}, f32[2,32]{1,0:T(2,128)}, u32[]{:S(2)}) copy-start(f32[2,32]{1,0:T(2,128)} %get-tuple-element.44) | copy-start | bytes 772
  164.6 72.1 %copy-start.28 = (f32[2,32]{1,0:T(2,128)S(1)}, f32[2,32]{1,0:T(2,128)}, u32[]{:S(2)}) copy-start(f32[2,32]{1,0:T(2,128)} %get-tuple-element.45) | copy-start | bytes 772
  164.6 72.1 %copy-start.29 = (f32[2,32]{1,0:T(2,128)S(1)}, f32[2,32]{1,0:T(2,128)}, u32[]{:S(2)}) copy-start(f32[2,32]{1,0:T(2,128)} %slice_multiply_fusion.2) | copy-start | bytes 772
  269.5 44.0 %all-to-all-start = ((bf16[2,256,4,1024]{3,1,0,2:T(8,128)(2,1)}), bf16[2,256,4,1024]{3,1,0,2:T(8,128)(2,1)}, u32[]{:S(2)}, u32[]{:S(2)}) async-start(bf16[2,256,4,1024]{3,1,0,2:T(8,128)(2,1)} %bitcast.138), calls=%async_computation | async-start | bytes 8388608 | tf_op jit(solution)/shard_map/all_to_all | solution.py:160
  (23 other events, 110.0 us)
Sparse Core Ops, SparseCore 0:
  10.2 96.2 all-gather.1

commit v3 on v0

--- a/solution.py
+++ b/solution.py
@@ -119,15 +119,16 @@
     small = jnp.concatenate(
         [passing, first_doc.astype(f32)[:, None], end_doc.astype(f32)[:, None]], axis=1
     )
-    received = []
-    for offset in range(reach, 0, -1):
-        got_small, got_state = shifted((small, own_state.astype(bf16)), "ctx", offset)
-        received.append(
-            (got_small[:, :heads], got_state.astype(f32), got_small[:, heads], got_small[:, heads + 1])
-        )
-    before = received[0]
-    for item in received[1:]:
-        before = link_states(before, item)
+    def send(summary, by):
+        tiny = jnp.concatenate([summary[0], summary[2][:, None], summary[3][:, None]], axis=1)
+        got_small, got_state = shifted((tiny, summary[1].astype(bf16)), "ctx", by)
+        return (got_small[:, :heads], got_state.astype(f32), got_small[:, heads], got_small[:, heads + 1])
+
+    own = (passing, own_state, first_doc.astype(f32), end_doc.astype(f32))
+    one_back = send(own, 1)
+    two_back = send(own, 2)
+    three_to_here = link_states(link_states(two_back, one_back), own)
+    before = link_states(send(three_to_here, 2), one_back)
 
     living = (doc_ids.astype(f32) == before[3][:, None]).astype(f32)
     carried = jnp.einsum(

time: 288 us -> 263 us (0.913)
  waiting for transfers between devices: 77.4 us -> 44.7 us
  starting transfers between devices: 72.7 us -> 58.7 us
  other arithmetic: 23.8 us -> 33.4 us
  matrix products: 41.1 us -> 47.4 us
  local copies, waits for them, and re-layouts: 55.3 us -> 61 us
    ppermute x20 -> x18, waiting for transfers between devices: 74.6 us -> 44 us  [shifted(): return lax.ppermute(value, axis, pairs)]
    ppermute x20 -> x18, starting transfers between devices: 72.6 us -> 58.6 us  [shifted(): return lax.ppermute(value, axis, pairs)]
    slice x1, other arithmetic: 0.78 us -> 6.47 us  [shards(): block_outs = [within[:, 0]]]
    convert_element_type x2 -> x3, other arithmetic: 2.05 us -> 6.68 us  [the longest x2 5.9 us: send(): got_small, got_state = shifted((tiny, summary[1].astype(bf16)), 'ctx', by)]
    dot_general x1, matrix products: 4.58 us -> 8.38 us  [shards(): jnp.einsum('bkhts,bkshp->bkthp', mixing, x, preferred_element_type=f32)]
    unnamed x43 -> x69, local copies, waits for them, and re-layouts: 21.2 us -> 22 us
  transfers between devices with their start and end apart: 22 -> 20, of which waited for: 8 -> 7; matrix products, arithmetic and copies ran while one was open for 36% -> 47% of each run, Pallas kernels for 0% -> 0%
where the time goes in v3:
time: 263 us; the launch traced here: 260 us
  local copies, waits for them, and re-layouts  61 us (23%)
  starting transfers between devices  58.7 us (22%)
  matrix products  47.4 us (18%)
  waiting for transfers between devices  44.7 us (17%)
  other arithmetic  33.4 us (13%)
  between operations  14.7 us (6%)
    ppermute x18, starting transfers between devices, shifted(): return lax.ppermute(value, axis, pairs)  58.6 us
    ppermute x18, waiting for transfers between devices, shifted(): return lax.ppermute(value, axis, pairs)  44 us
    unnamed x69, local copies, waits for them, and re-layouts  22 us
    dot_general x1, matrix products, shards(): jnp.einsum('btc,cd->btd', normed, lax.all_gather(out_weight, 'ctx', axis=...  14 us
    sub x1, matrix products, shards(): probs = jnp.where(allowed, jnp.exp(scores - top), 0.0)  13.4 us
    dot_general x1, matrix products, shards(): jnp.einsum('bkhts,bkshp->bkthp', mixing, x, preferred_element_type=f32)  8.38 us
    another operation x1, local copies, waits for them, and re-layouts, shards(): jnp.stack(block_outs, axis=1).reshape(batches, length, heads, P_SIZE)  8.03 us
    reshape x1, local copies, waits for them, and re-layouts, shards(): x = mixer_input.reshape(batches, count, SPAN, heads, P_SIZE)  7.18 us
  transfers between devices with their start and end apart: 20, of which 7 were waited for; matrix products, arithmetic and copies ran while one was open for 47% of the time, Pallas kernels for 0%

profile of v3, /device:TPU:9, one launch (start us, length us, event | category | flops | bytes accessed | tf_op | source)
XLA Modules:
  0.0 260.0 jit_solution(14246652677840130527)
XLA Ops:
  12.9 3.5 %collective-permute-start.1 = (f32[2,34]{1,0:T(2,128)}, f32[2,34]{1,0:T(2,128)}, u32[]{:S(2)}, u32[]{:S(2)}) collective-permute-start(f32[2,34]{1,0:T(2,128)} %pad_maximum_fusion.1), channel_id=1, source_target_pairs={{0,8},{4,12},{8,16},{12,20},{16,24},{20,28},{24,32},{28,36},{32,40... | collective-permute-start | bytes 824 | tf_op jit(solution)/shard_map/ppermute | solution.py:19
  16.4 4.4 %collective-permute-start.2 = (f32[2,34]{1,0:T(2,128)}, f32[2,34]{1,0:T(2,128)S(1)}, u32[]{:S(2)}, u32[]{:S(2)}) collective-permute-start(f32[2,34]{1,0:T(2,128)} %pad_maximum_fusion.1), channel_id=1, source_target_pairs={{0,4},{4,8},{8,12},{12,16},{16,20},{20,24},{24,28},{28,32},{32,36}... | collective-permute-start | bytes 824 | tf_op jit(solution)/shard_map/ppermute | solution.py:19
  26.8 3.6 %reshape.277 = f32[2,2,128,2,16,64]{2,1,5,4,3,0:T(2,128)} reshape(bf16[2,256,2048]{1,2,0:T(8,128)(2,1)S(1)} %copy.83) | data formatting | bytes 6291456 | tf_op jit(solution)/shard_map/convert_element_type | solution.py:89
  31.2 4.5 %multiply_convert_fusion.2 = bf16[2,2,128,2,16,64]{2,1,5,4,3,0:T(2,128)(2,1)S(1)} fusion(f32[2,2,128,2,16,64]{2,1,5,4,3,0:T(2,128)} %reshape.277, f32[2,2,128,2,16]{2,1,4,3,0:T(2,128)S(1)} %copy.82), kind=kLoop, calls=%fused_computation.32 | loop fusion | flops 2097152 | bytes 6356992 | tf_op jit(solution)/shard_map/convert_element_type | solution.py:89
  46.2 7.2 %reshape.289 = bf16[2,2,128,32,64]{4,3,2,1,0:T(8,128)(2,1)} reshape(bf16[2,256,2048]{2,1,0:T(8,128)(2,1)} %param.13) | data formatting | bytes 4194304 | tf_op jit(solution)/shard_map/reshape | solution.py:64
  59.1 3.4 %fusion.44 = f32[2,2,16,64,128]{4,3,2,1,0:T(8,128)} fusion(bf16[2,1,128,2,128]{4,3,2,1,0:T(2,128)(2,1)S(1)} %slice.106, f32[2,2,2,16,64,128]{5,4,3,2,1,0:T(8,128)} %copy-done), kind=kOutput, calls=%fused_computation.54 | convolution fusion | flops 134217728 | bytes 3276800 | tf_op jit(solution)/shard_map/btgn,bgrpn->btgrp/dot_general | solution.py:100
  64.7 8.4 %fusion.32 = f32[2,2,128,32,64]{2,4,3,1,0:T(8,128)} fusion(bf16[2,2,128,32,64]{4,3,2,1,0:T(8,128)(2,1)S(1)} %copy-done.7, f32[2,2,32,128,128]{4,3,2,1,0:T(8,128)S(1)} %bitcast.129, f32[2,2,32,128]{3,2,1,0:T(8,128)S(1)} %copy-done.17, f32[2,2,32,128]{3,2,1,0:T(8,128)S(1)} %copy.72, pred[2,2,128,128]{3,2,1,0:T(8,128)(4,1)S(1)} %compare_and_fusion.1), kind=kOutput, calls=%fused_computation.42 | convolution fusion | flops 283115520 | bytes 14876672 | tf_op jit(solution)/shard_map/bkhts,bkshp->bkthp/dot_general | solution.py:82
  74.8 6.5 %fusion.79 = (f32[2,1,128,32,64]{2,4,3,1,0:T(8,128)}, f32[2,1,128,32,64]{2,4,3,1,0:T(8,128)}) fusion(f32[2,2,128,32,64]{2,4,3,1,0:T(8,128)} %fusion.32, f32[2,1,128,32,64]{2,4,3,1,0:T(8,128)} %bitcast.128, f32[2,128,32]{1,2,0:T(8,128)S(1)} %copy.88), kind=kLoop, calls=%fused_computation.142 | loop fusion | flops 1048576 | bytes 10518528 | tf_op jit(solution)/shard_map/slice | solution.py:97
  82.0 4.0 %copy.93 = bf16[2,256,2048]{1,2,0:T(8,128)(2,1)} copy(bf16[2,256,2048]{2,1,0:T(8,128)(2,1)} %param.14) | data formatting | bytes 4194304 | tf_op args[1]
  87.6 24.4 %collective-permute-done.4 = bf16[2,32,64,128]{3,2,1,0:T(8,128)(2,1)} collective-permute-done((bf16[2,32,64,128]{3,2,1,0:T(8,128)(2,1)}, bf16[2,32,64,128]{3,2,1,0:T(8,128)(2,1)}, u32[]{:S(2)}, u32[]{:S(2)}) %collective-permute-start.4) | collective-permute-done | bytes 1048608 | tf_op jit(solution)/shard_map/ppermute | solution.py:19
  112.0 4.4 %fusion.37 = bf16[2,32,64,128]{3,2,1,0:T(8,128)(2,1)} fusion(bf16[2,32,64,128]{3,2,1,0:T(8,128)(2,1)S(1)} %collective-permute-done, bf16[2,32,64,128]{3,2,1,0:T(8,128)(2,1)} %collective-permute-done.4, f32[2,32]{1,0:T(2,128)S(1)} %get-tuple-element.16, f32[2,32]{1,0:T(2,128)S(1)} %get-tuple-element.15, f32[2,32,64,128]{3,2,1,0:T(8,128)} %bitcast.127, ...), kind=kLoop, calls=%fused_computation.45 | loop fusion | flops 4718592 | bytes 7340800 | tf_op jit(solution)/shard_map/convert_element_type | solution.py:124
  123.8 8.0 %copy.89 = f32[2,2,128,32,64]{2,1,4,3,0:T(2,128)} copy(f32[2,2,128,32,64]{2,4,3,1,0:T(8,128)} %pad_maximum_fusion) | data formatting | bytes 8388608 | tf_op jit(solution)/shard_map/stack | solution.py:112
  131.8 6.4 %reshape.268 = f32[2,256,2048]{1,2,0:T(8,128)} reshape(f32[2,2,128,32,64]{2,1,4,3,0:T(2,128)} %copy.89) | data formatting | bytes 8388608 | tf_op jit(solution)/shard_map/reshape | solution.py:112
  145.5 14.0 %fusion.12 = bf16[2,256,4096]{2,1,0:T(8,128)(2,1)} fusion(bf16[2,256,2048]{1,2,0:T(8,128)(2,1)S(1)} %fusion.23, bf16[2048,4096]{1,0:T(8,128)(2,1)} %all-gather.2.cloned.1.call-done), kind=kOutput, calls=%fused_computation.15 | convolution fusion | flops 8592031744 | bytes 23068672 | tf_op jit(solution)/shard_map/btc,cd->btd/dot_general | solution.py:147
  160.4 5.7 %collective-permute-start.14 = (bf16[2,256,256]{2,1,0:T(8,128)(2,1)S(1)}, bf16[2,256,256]{2,1,0:T(8,128)(2,1)}, u32[]{:S(2)}, u32[]{:S(2)}) collective-permute-start(bf16[2,256,256]{2,1,0:T(8,128)(2,1)S(1)} %copy-done.15), channel_id=1, source_target_pairs={{0,16},{4,20},{8,24},{12,28},{16,32},{20,36},{24,40},{28,44},{32,4... | collective-permute-start | bytes 786440 | tf_op jit(solution)/shard_map/ppermute | solution.py:19
  170.2 3.6 %collective-permute-start.17 = (bf16[2,256,256]{2,1,0:T(8,128)(2,1)S(1)}, bf16[2,256,256]{2,1,0:T(8,128)(2,1)S(1)}, u32[]{:S(2)}, u32[]{:S(2)}) collective-permute-start(bf16[2,256,256]{2,1,0:T(8,128)(2,1)S(1)} %copy-done.15), channel_id=1, source_target_pairs={{0,4},{4,8},{8,12},{12,16},{16,20},{20,24},{24,28},{28,32},{32,36}... | collective-permute-start | bytes 786440 | tf_op jit(solution)/shard_map/ppermute | solution.py:19
  173.9 4.4 %collective-permute-start.6 = (bf16[2,256]{1,0:T(2,128)(2,1)S(1)}, bf16[2,256]{1,0:T(2,128)(2,1)S(1)}, u32[]{:S(2)}, u32[]{:S(2)}) collective-permute-start(bf16[2,256]{1,0:T(2,128)(2,1)S(1)} %convert_element_type.131), channel_id=1, source_target_pairs={{0,16},{4,20},{8,24},{12,28},{16,32},{20,36},{24,40},{28,44},{32,4... | collective-permute-start | bytes 3080 | tf_op jit(solution)/shard_map/ppermute | solution.py:19
  180.2 3.3 %collective-permute-done.6 = bf16[2,256]{1,0:T(2,128)(2,1)S(1)} collective-permute-done((bf16[2,256]{1,0:T(2,128)(2,1)S(1)}, bf16[2,256]{1,0:T(2,128)(2,1)S(1)}, u32[]{:S(2)}, u32[]{:S(2)}) %collective-permute-start.6) | collective-permute-done | bytes 1056 | tf_op jit(solution)/shard_map/ppermute | solution.py:19
  185.7 4.8 %collective-permute-done.7 = bf16[2,256]{1,0:T(2,128)(2,1)S(1)} collective-permute-done((bf16[2,256]{1,0:T(2,128)(2,1)S(1)}, bf16[2,256]{1,0:T(2,128)(2,1)S(1)}, u32[]{:S(2)}, u32[]{:S(2)}) %collective-permute-start.7) | collective-permute-done | bytes 1056 | tf_op jit(solution)/shard_map/ppermute | solution.py:19
  197.0 3.3 %collective-permute-start.9 = (bf16[2,256]{1,0:T(2,128)(2,1)S(1)}, bf16[2,256]{1,0:T(2,128)(2,1)S(1)}, u32[]{:S(2)}, u32[]{:S(2)}) collective-permute-start(bf16[2,256]{1,0:T(2,128)(2,1)S(1)} %convert_element_type.131), channel_id=1, source_target_pairs={{0,4},{4,8},{8,12},{12,16},{16,20},{20,24},{24,28},{28,32},{32,36}... | collective-permute-start | bytes 3080 | tf_op jit(solution)/shard_map/ppermute | solution.py:19
  205.3 8.6 %collective-permute-start.11 = (bf16[2,256,256]{1,2,0:T(8,128)(2,1)S(1)}, bf16[2,256,256]{1,2,0:T(8,128)(2,1)}, u32[]{:S(2)}, u32[]{:S(2)}) collective-permute-start(bf16[2,256,256]{1,2,0:T(8,128)(2,1)S(1)} %copy.95), channel_id=1, source_target_pairs={{0,12},{4,16},{8,20},{12,24},{16,28},{20,32},{24,36},{28,40},{32,4... | collective-permute-start | bytes 786440 | tf_op jit(solution)/shard_map/ppermute | solution.py:19
  224.3 4.4 %collective-permute-done.12 = bf16[2,256,256]{1,2,0:T(8,128)(2,1)} collective-permute-done((bf16[2,256,256]{1,2,0:T(8,128)(2,1)S(1)}, bf16[2,256,256]{1,2,0:T(8,128)(2,1)}, u32[]{:S(2)}, u32[]{:S(2)}) %collective-permute-start.12) | collective-permute-done | bytes 262176 | tf_op jit(solution)/shard_map/ppermute | solution.py:19
  232.9 13.4 %fusion.81 = (f32[2,2,4,256]{3,2,1,0:T(4,128)S(1)}, bf16[2,2,4,256,1280]{3,4,2,1,0:T(8,128)(2,1)}) fusion(pred[2,256,1280]{1,2,0:T(8,128)(4,1)S(1)} %compare_and_fusion, bf16[2,1280,2,128,1]{1,3,4,2,0:T(8,128)(2,1)} %bitcast.139, bf16[2,256,2,4,128]{4,3,2,1,0:T(4,128)(2,1)S(1)} %copy-done.10), kind=kOutput, calls=%fused_computation.144 | convolution fusion | flops 2721056000 | bytes 13516800 | tf_op jit(solution)/shard_map/sub | solution.py:182
  246.3 5.5 %fusion.39 = bf16[2,256,2,4,128]{1,4,3,2,0:T(8,128)(2,1)S(1)} fusion(bf16[2,1280,2,128,1]{1,3,4,2,0:T(8,128)(2,1)S(1)} %bitcast.133, bf16[2,2,4,256,1280]{3,4,2,1,0:T(8,128)(2,1)} %get-tuple-element.28, f32[2,256,2,4]{1,3,2,0:T(4,128)S(1)} %bitcast.145), kind=kOutput, calls=%fused_computation.49 | convolution fusion | flops 1343225856 | bytes 12861440 | tf_op jit(solution)/shard_map/bgrqk,bkgd->bgrqd/dot_general | solution.py:184
  (171 shorter events, 85.6 us)
Async XLA Ops:
  7.2 138.4 %all-gather.2.cloned.1.call-start = ((), (), s32[]{:S(2)}) async-start(), calls=%async_computation.1 | async-start | bytes 17301504 | tf_op jit(solution)/shard_map/all_gather | solution.py:150
  7.9 245.3 %reduce-scatter.2.cloned.1.call-start = ((), (), s32[]{:S(2)}) async-start(), calls=%async_computation.2 | async-start | bytes 5242880 | tf_op jit(solution)/shard_map/reduce_scatter | solution.py:153
  12.9 73.1 %collective-permute-start.1 = (f32[2,34]{1,0:T(2,128)}, f32[2,34]{1,0:T(2,128)}, u32[]{:S(2)}, u32[]{:S(2)}) collective-permute-start(f32[2,34]{1,0:T(2,128)} %pad_maximum_fusion.1), channel_id=1, source_target_pairs={{0,8},{4,12},{8,16},{12,20},{16,24},{20,28},{24,32},{28,36},{32,40... | collective-permute-start | bytes 824 | tf_op jit(solution)/shard_map/ppermute | solution.py:19
  16.4 69.5 %collective-permute-start.2 = (f32[2,34]{1,0:T(2,128)}, f32[2,34]{1,0:T(2,128)S(1)}, u32[]{:S(2)}, u32[]{:S(2)}) collective-permute-start(f32[2,34]{1,0:T(2,128)} %pad_maximum_fusion.1), channel_id=1, source_target_pairs={{0,4},{4,8},{8,12},{12,16},{16,20},{20,24},{24,28},{28,32},{32,36}... | collective-permute-start | bytes 824 | tf_op jit(solution)/shard_map/ppermute | solution.py:19
  40.8 16.8 %copy-start.16 = (s32[2,256]{1,0:T(2,128)S(1)}, s32[2,256]{1,0:T(2,128)}, u32[]{:S(2)}) copy-start(s32[2,256]{1,0:T(2,128)} %param.25) | copy-start | bytes 6148
  40.8 46.8 %collective-permute-start = (bf16[2,32,64,128]{3,2,1,0:T(8,128)(2,1)}, bf16[2,32,64,128]{3,2,1,0:T(8,128)(2,1)S(1)}, u32[]{:S(2)}, u32[]{:S(2)}) collective-permute-start(bf16[2,32,64,128]{3,2,1,0:T(8,128)(2,1)} %fusion.54), channel_id=1, source_target_pairs={{0,4},{4,8},{8,12},{12,16},{16,20},{20,24},{24,28},{28,32},{32,36}... | collective-permute-start | bytes 3145736 | tf_op jit(solution)/shard_map/ppermute | solution.py:19
  42.9 69.1 %collective-permute-start.4 = (bf16[2,32,64,128]{3,2,1,0:T(8,128)(2,1)}, bf16[2,32,64,128]{3,2,1,0:T(8,128)(2,1)}, u32[]{:S(2)}, u32[]{:S(2)}) collective-permute-start(bf16[2,32,64,128]{3,2,1,0:T(8,128)(2,1)} %fusion.54), channel_id=1, source_target_pairs={{0,8},{4,12},{8,16},{12,20},{16,24},{20,28},{24,32},{28,36},{32,40... | collective-permute-start | bytes 3145736 | tf_op jit(solution)/shard_map/ppermute | solution.py:19
  82.0 30.0 %copy-start.22 = (f32[2,32]{1,0:T(2,128)S(1)}, f32[2,32]{1,0:T(2,128)}, u32[]{:S(2)}) copy-start(f32[2,32]{1,0:T(2,128)} %copy-done.21) | copy-start | bytes 772
  116.3 22.4 %collective-permute-start.5 = (bf16[2,32,64,128]{3,2,1,0:T(8,128)(2,1)}, bf16[2,32,64,128]{3,2,1,0:T(8,128)(2,1)}, u32[]{:S(2)}, u32[]{:S(2)}) collective-permute-start(bf16[2,32,64,128]{3,2,1,0:T(8,128)(2,1)} %fusion.37), channel_id=1, source_target_pairs={{0,8},{4,12},{8,16},{12,20},{16,24},{20,28},{24,32},{28,36},{32,40... | collective-permute-start | bytes 3145736 | tf_op jit(solution)/shard_map/ppermute | solution.py:19
  120.9 17.4 %collective-permute-start.3 = (f32[2,34]{1,0:T(2,128)S(1)}, f32[2,34]{1,0:T(2,128)S(1)}, u32[]{:S(2)}, u32[]{:S(2)}) collective-permute-start(f32[2,34]{1,0:T(2,128)S(1)} %pad_maximum_fusion.2), channel_id=1, source_target_pairs={{0,8},{4,12},{8,16},{12,20},{16,24},{20,28},{24,32},{28,36},{32,40... | collective-permute-start | bytes 824 | tf_op jit(solution)/shard_map/ppermute | solution.py:19
  159.5 19.0 %copy-start.14 = (bf16[2,256,256]{2,1,0:T(8,128)(2,1)S(1)}, bf16[2,256,256]{2,1,0:T(8,128)(2,1)}, u32[]{:S(2)}) copy-start(bf16[2,256,256]{2,1,0:T(8,128)(2,1)} %param.23) | copy-start | bytes 786436
  159.5 19.2 %copy-start.9 = (bf16[2,256,1024]{2,1,0:T(8,128)(2,1)S(1)}, bf16[2,256,1024]{2,1,0:T(8,128)(2,1)}, u32[]{:S(2)}) copy-start(bf16[2,256,1024]{2,1,0:T(8,128)(2,1)} %param.22) | copy-start | bytes 3145732
  160.4 44.9 %collective-permute-start.14 = (bf16[2,256,256]{2,1,0:T(8,128)(2,1)S(1)}, bf16[2,256,256]{2,1,0:T(8,128)(2,1)}, u32[]{:S(2)}, u32[]{:S(2)}) collective-permute-start(bf16[2,256,256]{2,1,0:T(8,128)(2,1)S(1)} %copy-done.15), channel_id=1, source_target_pairs={{0,16},{4,20},{8,24},{12,28},{16,32},{20,36},{24,40},{28,44},{32,4... | collective-permute-start | bytes 786440 | tf_op jit(solution)/shard_map/ppermute | solution.py:19
  166.2 48.8 %collective-permute-start.15 = (bf16[2,256,256]{2,1,0:T(8,128)(2,1)S(1)}, bf16[2,256,256]{2,1,0:T(8,128)(2,1)}, u32[]{:S(2)}, u32[]{:S(2)}) collective-permute-start(bf16[2,256,256]{2,1,0:T(8,128)(2,1)S(1)} %copy-done.15), channel_id=1, source_target_pairs={{0,12},{4,16},{8,20},{12,24},{16,28},{20,32},{24,36},{28,40},{32,4... | collective-permute-start | bytes 786440 | tf_op jit(solution)/shard_map/ppermute | solution.py:19
  168.3 49.6 %collective-permute-start.16 = (bf16[2,256,256]{2,1,0:T(8,128)(2,1)S(1)}, bf16[2,256,256]{2,1,0:T(8,128)(2,1)S(1)}, u32[]{:S(2)}, u32[]{:S(2)}) collective-permute-start(bf16[2,256,256]{2,1,0:T(8,128)(2,1)S(1)} %copy-done.15), channel_id=1, source_target_pairs={{0,8},{4,12},{8,16},{12,20},{16,24},{20,28},{24,32},{28,36},{32,40... | collective-permute-start | bytes 786440 | tf_op jit(solution)/shard_map/ppermute | solution.py:19
  170.2 49.6 %collective-permute-start.17 = (bf16[2,256,256]{2,1,0:T(8,128)(2,1)S(1)}, bf16[2,256,256]{2,1,0:T(8,128)(2,1)S(1)}, u32[]{:S(2)}, u32[]{:S(2)}) collective-permute-start(bf16[2,256,256]{2,1,0:T(8,128)(2,1)S(1)} %copy-done.15), channel_id=1, source_target_pairs={{0,4},{4,8},{8,12},{12,16},{16,20},{20,24},{24,28},{28,32},{32,36}... | collective-permute-start | bytes 786440 | tf_op jit(solution)/shard_map/ppermute | solution.py:19
  173.9 9.7 %collective-permute-start.6 = (bf16[2,256]{1,0:T(2,128)(2,1)S(1)}, bf16[2,256]{1,0:T(2,128)(2,1)S(1)}, u32[]{:S(2)}, u32[]{:S(2)}) collective-permute-start(bf16[2,256]{1,0:T(2,128)(2,1)S(1)} %convert_element_type.131), channel_id=1, source_target_pairs={{0,16},{4,20},{8,24},{12,28},{16,32},{20,36},{24,40},{28,44},{32,4... | collective-permute-start | bytes 3080 | tf_op jit(solution)/shard_map/ppermute | solution.py:19
  183.5 7.0 %collective-permute-start.7 = (bf16[2,256]{1,0:T(2,128)(2,1)S(1)}, bf16[2,256]{1,0:T(2,128)(2,1)S(1)}, u32[]{:S(2)}, u32[]{:S(2)}) collective-permute-start(bf16[2,256]{1,0:T(2,128)(2,1)S(1)} %convert_element_type.131), channel_id=1, source_target_pairs={{0,12},{4,16},{8,20},{12,24},{16,28},{20,32},{24,36},{28,40},{32,4... | collective-permute-start | bytes 3080 | tf_op jit(solution)/shard_map/ppermute | solution.py:19
  190.5 6.4 %collective-permute-start.8 = (bf16[2,256]{1,0:T(2,128)(2,1)S(1)}, bf16[2,256]{1,0:T(2,128)(2,1)S(1)}, u32[]{:S(2)}, u32[]{:S(2)}) collective-permute-start(bf16[2,256]{1,0:T(2,128)(2,1)S(1)} %convert_element_type.131), channel_id=1, source_target_pairs={{0,8},{4,12},{8,16},{12,20},{16,24},{20,28},{24,32},{28,36},{32,40... | collective-permute-start | bytes 3080 | tf_op jit(solution)/shard_map/ppermute | solution.py:19
  197.0 5.8 %collective-permute-start.9 = (bf16[2,256]{1,0:T(2,128)(2,1)S(1)}, bf16[2,256]{1,0:T(2,128)(2,1)S(1)}, u32[]{:S(2)}, u32[]{:S(2)}) collective-permute-start(bf16[2,256]{1,0:T(2,128)(2,1)S(1)} %convert_element_type.131), channel_id=1, source_target_pairs={{0,4},{4,8},{8,12},{12,16},{16,20},{20,24},{24,28},{28,32},{32,36}... | collective-permute-start | bytes 3080 | tf_op jit(solution)/shard_map/ppermute | solution.py:19
  202.7 17.2 %collective-permute-start.10 = (bf16[2,256,256]{1,2,0:T(8,128)(2,1)S(1)}, bf16[2,256,256]{1,2,0:T(8,128)(2,1)S(1)}, u32[]{:S(2)}, u32[]{:S(2)}) collective-permute-start(bf16[2,256,256]{1,2,0:T(8,128)(2,1)S(1)} %copy.95), channel_id=1, source_target_pairs={{0,16},{4,20},{8,24},{12,28},{16,32},{20,36},{24,40},{28,44},{32,4... | collective-permute-start | bytes 786440 | tf_op jit(solution)/shard_map/ppermute | solution.py:19
  205.3 17.3 %collective-permute-start.11 = (bf16[2,256,256]{1,2,0:T(8,128)(2,1)S(1)}, bf16[2,256,256]{1,2,0:T(8,128)(2,1)}, u32[]{:S(2)}, u32[]{:S(2)}) collective-permute-start(bf16[2,256,256]{1,2,0:T(8,128)(2,1)S(1)} %copy.95), channel_id=1, source_target_pairs={{0,12},{4,16},{8,20},{12,24},{16,28},{20,32},{24,36},{28,40},{32,4... | collective-permute-start | bytes 786440 | tf_op jit(solution)/shard_map/ppermute | solution.py:19
  215.0 13.7 %collective-permute-start.12 = (bf16[2,256,256]{1,2,0:T(8,128)(2,1)S(1)}, bf16[2,256,256]{1,2,0:T(8,128)(2,1)}, u32[]{:S(2)}, u32[]{:S(2)}) collective-permute-start(bf16[2,256,256]{1,2,0:T(8,128)(2,1)S(1)} %copy.95), channel_id=1, source_target_pairs={{0,8},{4,12},{8,16},{12,20},{16,24},{20,28},{24,32},{28,36},{32,40... | collective-permute-start | bytes 786440 | tf_op jit(solution)/shard_map/ppermute | solution.py:19
  217.9 12.6 %collective-permute-start.13 = (bf16[2,256,256]{1,2,0:T(8,128)(2,1)S(1)}, bf16[2,256,256]{1,2,0:T(8,128)(2,1)}, u32[]{:S(2)}, u32[]{:S(2)}) collective-permute-start(bf16[2,256,256]{1,2,0:T(8,128)(2,1)S(1)} %copy.95), channel_id=1, source_target_pairs={{0,4},{4,8},{8,12},{12,16},{16,20},{20,24},{24,28},{28,32},{32,36}... | collective-permute-start | bytes 786440 | tf_op jit(solution)/shard_map/ppermute | solution.py:19
  (24 other events, 104.6 us)
Sparse Core Ops, SparseCore 0:
  10.1 111.7 all-gather.1
  159.6 47.7 reduce-scatter.1
